TPU v7x, 512 devices: a whole 4x4x16 slice. The times are simulated.
512 devices in a mesh: src: 16 (over z_hi, x), dst: 32 (over z_lo, y, core).
Axes of the slice: x: 4, y: 4, z: 16 (z_hi: 4, z_lo: 4; z = z_hi * 4 + z_lo), core: 2. Of those that a mesh axis runs over, the one named last changes fastest.
Arguments:
- rel_ops: bfloat16 [2048, 400, 400], P(('src', 'dst')), may hold values from -0.3125 to 0.3125
- src_emb: bfloat16 [4096, 400], P('src'), may hold values from -1.796875 to 1.796875
- dst_emb: bfloat16 [8192, 400], P('dst'), may hold values from -6 to 6
- edge_src: int32 [16, 32, 1024], P('src', 'dst'), may hold values from 0 to 255
- edge_dst: int32 [16, 32, 1024], P('src', 'dst'), may hold values from 0 to 255
- slot_count: int32 [16, 32, 64], P('src', 'dst'), may hold values from 0 to 16
- neg_span: int32 [16, 2], P('src'), may hold values from 0 to 31
Outputs:
- grad_rel: bfloat16 [2048, 400, 400], P(('src', 'dst'))
- grad_src: bfloat16 [4096, 400], P('src')
- grad_dst: bfloat16 [8192, 400], P('dst')
All inputs are finite; a program needn't handle non-finite values.
Results may differ from a plain program's by a relative error of at most 0.015.
Values may be sent and summed in bfloat16 or wider, within the bound.
No kernel may reach another device: no remote copies, remote signals or barrier semaphores. Data moves between devices by JAX's collectives and lax.ppermute only.
A program may use at most 64 MiB of HBM per device.

v0:
```python
import jax
import jax.numpy as jnp
from jax import lax
from jax.sharding import PartitionSpec as P


def from_root(block, axis, holder):
    block = jnp.where(lax.axis_index(axis) == holder, block, jnp.zeros_like(block))
    return lax.psum(block, axis)


def send_back(rows_out):
    return lax.all_to_all(rows_out, "src", split_axis=0, concat_axis=0, tiled=True)


def body(rel_ops, src_emb, dst_emb, edge_src, edge_dst, slot_count, neg_span):
    n_src = lax.axis_size("src")
    rel_count = rel_ops.shape[0]
    model_width = rel_ops.shape[1]
    part_rows = src_emb.shape[0]
    slot_total = edge_src.shape[2]
    slot_cap = slot_total // (n_src * rel_count)
    ids_src = edge_src.reshape(slot_total)
    ids_dst = edge_dst.reshape(slot_total)
    counts = slot_count.reshape(n_src * rel_count)
    slot_lane = jnp.arange(slot_total, dtype=jnp.int32) % slot_cap
    live_mask = (slot_lane < jnp.repeat(counts, slot_cap, total_repeat_length=slot_total)).astype(
        jnp.float32
    )
    inputs = src_emb[ids_src].reshape(n_src, rel_count, slot_cap, model_width)
    received = lax.all_to_all(inputs, "src", split_axis=0, concat_axis=0, tiled=True)
    applied = jnp.einsum(
        "skcd,kde->skce", received, rel_ops, preferred_element_type=jnp.float32
    ).astype(jnp.bfloat16)
    mapped = lax.all_to_all(applied, "src", split_axis=0, concat_axis=0, tiled=True)
    mapped_rows = mapped.reshape(slot_total, model_width)
    targets = dst_emb[ids_dst]
    span_ids = neg_span.reshape(-1)
    span_total = span_ids.shape[0]
    pieces = [from_root(dst_emb, "dst", span_ids[index]) for index in range(span_total)]
    negatives = jnp.concatenate(pieces, 0)
    block_rows = min(512, slot_total)
    block_count = slot_total // block_rows

    def block_step(span_acc, block_in):
        rows_z, rows_y, rows_live = block_in
        neg_score = jnp.einsum("bd,nd->bn", rows_z, negatives, preferred_element_type=jnp.float32)
        pos_score = jnp.sum(rows_z.astype(jnp.float32) * rows_y.astype(jnp.float32), -1)
        row_max = jnp.maximum(jnp.max(neg_score, -1), pos_score)
        exp_neg = jnp.exp(neg_score - row_max[:, None])
        exp_pos = jnp.exp(pos_score - row_max)
        denom = jnp.sum(exp_neg, -1) + exp_pos
        grad_neg = (exp_neg * (rows_live / denom)[:, None]).astype(jnp.bfloat16)
        grad_pos = (exp_pos / denom - 1.0) * rows_live
        upstream = grad_pos[:, None] * rows_y.astype(jnp.float32) + jnp.dot(
            grad_neg, negatives, preferred_element_type=jnp.float32
        )
        dst_term = grad_pos[:, None] * rows_z.astype(jnp.float32)
        span_acc = span_acc + jnp.einsum(
            "bn,bd->nd", grad_neg, rows_z, preferred_element_type=jnp.float32
        )
        return (span_acc, (upstream.astype(jnp.bfloat16), dst_term))

    span_start = jnp.zeros((span_total * part_rows, model_width), jnp.float32)
    scanned = (
        mapped_rows.reshape(block_count, block_rows, model_width),
        targets.reshape(block_count, block_rows, model_width),
        live_mask.reshape(block_count, block_rows),
    )
    span_grad, (up_blocks, dst_blocks) = lax.scan(block_step, span_start, scanned)
    grads_out = up_blocks.reshape(n_src, rel_count, slot_cap, model_width)
    received = (
        lax.all_to_all(grads_out, "src", split_axis=0, concat_axis=0, tiled=True),
        lax.all_to_all(inputs, "src", split_axis=0, concat_axis=0, tiled=True),
    )
    grads_in = send_back(
        jnp.einsum(
            "skce,kde->skcd", received[0], rel_ops, preferred_element_type=jnp.float32
        ).astype(jnp.bfloat16)
    )
    grads_recv = received[0]
    inputs_recv = received[1]
    grad_rel = jnp.einsum(
        "skcd,skce->kde", inputs_recv, grads_recv, preferred_element_type=jnp.float32
    ).astype(jnp.bfloat16)
    src_local = jax.ops.segment_sum(
        grads_in.reshape(slot_total, model_width).astype(jnp.float32),
        ids_src,
        num_segments=part_rows,
    )
    grad_src = lax.psum(src_local, "dst").astype(jnp.bfloat16)
    span_sums = (
        lax.psum(span_grad.astype(jnp.bfloat16), "dst")
        .astype(jnp.float32)
        .reshape(span_total, part_rows, model_width)
    )
    own_index = lax.axis_index("dst")
    dst_local = jax.ops.segment_sum(
        dst_blocks.reshape(slot_total, model_width), ids_dst, num_segments=part_rows
    )
    for index in range(span_total):
        dst_local = dst_local + jnp.where(span_ids[index] == own_index, span_sums[index], 0.0)
    grad_dst = lax.psum(dst_local, "src").astype(jnp.bfloat16)
    return (grad_rel, grad_src, grad_dst)


def solution(mesh):
    placed = (
        P(("src", "dst"), None, None),
        P("src", None),
        P("dst", None),
        P("src", "dst", None),
        P("src", "dst", None),
        P("src", "dst", None),
        P("src", None),
    )
    return jax.shard_map(
        body,
        mesh=mesh,
        in_specs=placed,
        out_specs=(P(("src", "dst"), None, None), P("src", None), P("dst", None)),
        check_vma=False,
    )
```

profile of v0, /device:TPU:1, one launch (start us, length us, event | category | flops | bytes accessed | tf_op | source)
XLA Modules:
  0.0 1052.6 jit_solution(10922361248387512830)
XLA Ops:
  8.0 1.1 copy.68
  9.1 5.1 gather_fusion
  14.2 67.0 %all_to_all.21 = bf16[16,4,16,400]{3,2,1,0:T(8,128)(2,1)S(1)} all-to-all(bf16[16,4,16,400]{3,2,1,0:T(8,128)(2,1)} %bitcast.146), channel_id=1, replica_groups=mesh['src'=16,'dst'=32] {'src'}, dimensions={0} | all-to-all | bytes 1638400 | tf_op jit(solution)/shard_map/all_to_all | solution.py:74
  82.1 1.1 copy.70
  83.2 11.6 %all-to-all-start.1 = ((bf16[16,4,16,400]{3,2,1,0:T(8,128)(2,1)}), bf16[16,4,16,400]{3,2,1,0:T(8,128)(2,1)}, u32[]{:S(2)}, u32[]{:S(2)}) async-start(bf16[16,4,16,400]{3,2,1,0:T(8,128)(2,1)} %copy.70), calls=%async_computation.1 | async-start | bytes 2097152 | tf_op jit(solution)/shard_map/all_to_all | solution.py:35
  100.8 4.3 compare_select_fusion.3
  105.8 35.6 %select_select_fusion = s32[1024]{0:T(1024)S(1)} fusion(pred[1024]{0:T(1024)(128)(4,1)S(1)} %get-tuple-element.256, pred[1024]{0:T(1024)(128)(4,1)S(1)} %get-tuple-element.255, pred[1024]{0:T(1024)(128)(4,1)S(1)} %get-tuple-element.254, pred[1024]{0:T(1024)(128)(4,1)S(1)} %get-tuple-element.253, pred[1024]{0:T(1024)(128)(4,1)S(1)} %get-tuple-element.252, ...), kind=kLoop, calls=%fused_computation.120 | loop fusion | flops 58368 | bytes 66788 | tf_op jit(solution)/shard_map/jit(_take)/gather | solution.py:27
  141.5 5.1 gather_fusion.1
  146.6 2.2 copy.75
  148.8 264.6 %all-reduce.8.cloned.1.call-done = (bf16[256,400]{1,0:T(8,128)(2,1)}, bf16[256,400]{1,0:T(8,128)(2,1)}) async-done(((bf16[256,400]{1,0:T(8,128)(2,1)}, bf16[256,400]{1,0:T(8,128)(2,1)}), (bf16[256,400]{1,0:T(8,128)(2,1)}, bf16[256,400]{1,0:T(8,128)(2,1)})) %all-reduce.8.cloned.1.call-update) | async-done | bytes 409616 | tf_op jit(solution)/shard_map/psum | solution.py:9
  413.4 1.9 pad_maximum_fusion
  415.2 1.4 copy.74
  416.7 15.8 %while.18 = (s32[]{:T(128)}, f32[512,400]{0,1:T(8,128)S(1)}, bf16[2,512,400]{1,2,0:T(8,128)(2,1)}, f32[2,512,400]{1,2,0:T(8,128)}, bf16[2,512,400]{1,2,0:T(8,128...) while((s32[]{:T(128)}, f32[512,400]{0,1:T(8,128)S(1)}, ...), condition=%wide.region_6.7_spmd.clone, body=%wide.region_2.6_spmd.clone.sunk | while | flops 633964544 | bytes 35072312 | solution.py:70
  416.7 1.2 fusion.56
  417.8 1.5 fusion.55
  421.6 1.0 copy-done.4
  423.4 1.2 copy-done.5
  424.6 1.1 fusion.56
  425.7 1.5 fusion.55
  431.3 1.2 copy-done.5
  432.5 2.2 copy.76
  434.7 47.1 %all_to_all.22 = bf16[16,4,16,400]{3,2,1,0:T(8,128)(2,1)S(1)} all-to-all(bf16[16,4,16,400]{3,2,1,0:T(8,128)(2,1)} %bitcast.147), channel_id=1, replica_groups=mesh['src'=16,'dst'=32] {'src'}, dimensions={0} | all-to-all | bytes 1638400 | tf_op jit(solution)/shard_map/all_to_all | solution.py:73
  482.8 1.1 copy.78
  483.9 6.4 all-to-all-start.3
  492.4 2.9 copy.86
  495.3 287.4 %all-reduce.6.cloned.1.call-done = bf16[512,400]{0,1:T(8,128)(2,1)} async-done(((bf16[512,400]{0,1:T(8,128)(2,1)}), bf16[512,400]{0,1:T(8,128)(2,1)}) %all-reduce.6.cloned.1.call-update) | async-done | bytes 409616 | tf_op jit(solution)/shard_map/psum | solution.py:93
  782.6 1.1 convert_element_type.82
  784.0 7.5 scatter_fusion
  791.5 99.3 %all-reduce.9 = bf16[256,400]{1,0:T(8,128)(2,1)S(1)} all-reduce(f32[256,400]{1,0:T(8,128)S(1)} %scatter_fusion), channel_id=1, replica_groups=mesh['src'=16,'dst'=32] {'src'}, use_global_device_ids=true, to_apply=%region_11.12 | all-reduce | flops 102400 | bytes 614400 | tf_op jit(solution)/shard_map/psum | solution.py:103
  891.6 3.3 bitcast_convert_fusion
  894.9 7.3 scatter_custom_fusion
  902.3 142.7 %all-reduce.10 = bf16[256,400]{1,0:T(8,128)(2,1)S(1)} all-reduce(f32[256,400]{1,0:T(8,128)S(1)} %scatter_custom_fusion), channel_id=1, replica_groups=mesh['src'=16,'dst'=32] {'dst'}, use_global_device_ids=true, to_apply=%region_8.9 | all-reduce | flops 102400 | bytes 614400 | tf_op jit(solution)/shard_map/psum | solution.py:91
  (83 shorter events, 18.0 us)
Async XLA Ops:
  7.2 74.0 %copy-start = (bf16[4,400,400]{2,1,0:T(8,128)(2,1)S(1)}, bf16[4,400,400]{2,1,0:T(8,128)(2,1)}, u32[]{:S(2)}) copy-start(bf16[4,400,400]{2,1,0:T(8,128)(2,1)} %param.11) | copy-start | bytes 3840004
  81.1 1.0 copy-start.6
  82.1 12.8 %copy-start.13 = (s32[1,2]{1,0:T(1,128)S(1)}, s32[1,2]{1,0:T(1,128)}, u32[]{:S(2)}) copy-start(s32[1,2]{1,0:T(1,128)} %param.17) | copy-start | bytes 28
  82.1 14.6 %copy-start.10 = (bf16[256,400]{0,1:T(8,128)(2,1)S(1)}, bf16[256,400]{0,1:T(8,128)(2,1)}, u32[]{:S(2)}) copy-start(bf16[256,400]{0,1:T(8,128)(2,1)} %param.13) | copy-start | bytes 614404
  83.2 14.6 %copy-start.3 = (s32[1,1,64]{2,1,0:T(1,128)S(1)}, s32[1,1,64]{2,1,0:T(1,128)}, u32[]{:S(2)}) copy-start(s32[1,1,64]{2,1,0:T(1,128)} %param.16) | copy-start | bytes 772
  83.2 17.5 %copy-start.12 = (s32[8,128]{1,0:T(8,128)S(1)}, s32[8,128]{1,0:T(8,128)}, u32[]{:S(2)}) copy-start(s32[8,128]{1,0:T(8,128)} %constant.161.clone.1) | copy-start | bytes 12292
  83.2 332.0 %all-to-all-start.1 = ((bf16[16,4,16,400]{3,2,1,0:T(8,128)(2,1)}), bf16[16,4,16,400]{3,2,1,0:T(8,128)(2,1)}, u32[]{:S(2)}, u32[]{:S(2)}) async-start(bf16[16,4,16,400]{3,2,1,0:T(8,128)(2,1)} %copy.70), calls=%async_computation.1 | async-start | bytes 2097152 | tf_op jit(solution)/shard_map/all_to_all | solution.py:35
  94.9 46.6 %copy-start.11 = (s32[1,1,1024]{2,1,0:T(1,128)S(1)}, s32[1,1,1024]{2,1,0:T(1,128)}, u32[]{:S(2)}) copy-start(s32[1,1,1024]{2,1,0:T(1,128)} %param.15) | copy-start | bytes 12292
  94.9 318.5 %all-reduce.8.cloned.1.call-start = ((), (), s32[]{:S(2)}) async-start(), calls=%async_computation.5 | async-start | bytes 1048576 | tf_op jit(solution)/shard_map/psum | solution.py:9
  419.5 1.0 copy-start.1
  419.6 1.3 copy-start.2
  419.6 1.5 copy-start.8
  421.1 1.4 copy-start.4
  422.5 0.9 copy-start.9
  423.4 1.2 copy-start.5
  427.4 1.0 copy-start.1
  427.5 1.3 copy-start.2
  427.5 1.5 copy-start.8
  429.0 1.4 copy-start.4
  430.4 0.9 copy-start.9
  431.3 1.2 copy-start.5
  481.8 1.0 copy-start.7
  483.9 411.0 %all-to-all-start.3 = ((bf16[16,4,16,400]{3,2,1,0:T(8,128)(2,1)}), bf16[16,4,16,400]{3,2,1,0:T(8,128)(2,1)}, u32[]{:S(2)}, u32[]{:S(2)}) async-start(bf16[16,4,16,400]{3,2,1,0:T(8,128)(2,1)} %copy.78), calls=%async_computation.3 | async-start | bytes 2097152 | tf_op jit(solution)/shard_map/all_to_all | solution.py:13
  490.3 292.3 %all-reduce.6.cloned.1.call-start = ((), (), s32[]{:S(2)}) async-start(), calls=%async_computation.4 | async-start | bytes 819200 | tf_op jit(solution)/shard_map/psum | solution.py:93
Sparse Core Ops, SparseCore 0:
  98.6 314.6 all-reduce.7
  494.0 288.5 all-reduce.5
where the time goes:
time: 1060 us; the launch traced here: 1050 us
  waiting for transfers between devices  552 us (52%)
  blocking collectives  356 us (34%)
  other arithmetic  64 us (6%)
  local copies, waits for them, and re-layouts  35.9 us (3%)
  starting transfers between devices  18.1 us (2%)
  between operations  16.7 us (2%)
    psum x1, waiting for transfers between devices, body(): lax.psum(span_grad.astype(jnp.bfloat16), 'dst').astype(jnp.float32)  287 us
    psum x1, waiting for transfers between devices, from_root(): return lax.psum(block, axis)  265 us
    psum x1, blocking collectives, body(): grad_src = lax.psum(src_local, 'dst').astype(jnp.bfloat16)  143 us
    psum x1, blocking collectives, body(): grad_dst = lax.psum(dst_local, 'src').astype(jnp.bfloat16)  99.3 us
    all_to_all x1, blocking collectives, body(): lax.all_to_all(inputs, 'src', split_axis=0, concat_axis=0, tiled=True)  67 us
    all_to_all x1, blocking collectives, body(): lax.all_to_all(grads_out, 'src', split_axis=0, concat_axis=0, tiled=True)  47.1 us
    gather x3, other arithmetic, body(): jnp.repeat(counts, slot_cap, total_repeat_length=slot_total)  40.7 us
  transfers between devices with their start and end apart: 4, of which 2 were waited for; matrix products, arithmetic and copies ran while one was open for 7% of the time, Pallas kernels for 0%

commit v1 on v0

v1 whole, which is shorter than its diff:
```python
import jax
import jax.numpy as jnp
from jax import lax
from jax.sharding import PartitionSpec as P

F32 = jnp.float32
BF16 = jnp.bfloat16


def butterfly_sum(x, axis, bits):
    n = lax.axis_size(axis)
    for bit in bits:
        low = x.astype(BF16)
        other = lax.ppermute(low, axis, [(i, i ^ bit) for i in range(n)])
        x = low.astype(F32) + other.astype(F32)
    return x


def axis_bits(n):
    return [1 << b for b in range(n.bit_length() - 1)]


def softmax_grads(z, y, negs, live):
    neg = jnp.einsum("...md,...nd->...mn", z, negs, preferred_element_type=F32)
    pos = jnp.sum(z.astype(F32) * y.astype(F32), -1)
    row_max = jnp.maximum(jnp.max(neg, -1), pos)
    exp_neg = jnp.exp(neg - row_max[..., None])
    exp_pos = jnp.exp(pos - row_max)
    denom = jnp.sum(exp_neg, -1) + exp_pos
    g_neg = (exp_neg * (live / denom)[..., None]).astype(BF16)
    g_pos = (exp_pos / denom - 1.0) * live
    return g_neg, g_pos


def body(rel_ops, src_emb, dst_emb, edge_src, edge_dst, slot_count, neg_span):
    n_src = lax.axis_size("src")
    n_dst = lax.axis_size("dst")
    rk = rel_ops.shape[0]
    width = rel_ops.shape[1]
    part = src_emb.shape[0]
    slots = edge_src.shape[2]
    cap = slots // (n_src * rk)
    nch = neg_span.shape[1]
    group = rk * cap
    ids_src = edge_src.reshape(slots)
    ids_dst = edge_dst.reshape(slots)
    counts = slot_count.reshape(n_src * rk)
    spans = neg_span.reshape(nch)
    own_dst = lax.axis_index("dst")

    every_dst = lax.all_gather(dst_emb, "dst", tiled=False)

    meta = jnp.concatenate(
        [
            jnp.broadcast_to(spans[None, :], (n_src, nch)),
            counts.reshape(n_src, rk),
            ids_dst.reshape(n_src, group),
        ],
        axis=1,
    ).astype(BF16)
    meta = jnp.pad(meta, ((0, 0), (0, width - meta.shape[1])))
    inputs = src_emb[ids_src].reshape(n_src, group, width)
    payload = jnp.concatenate([inputs, meta[:, None, :]], axis=1)
    received = lax.all_to_all(payload, "src", 0, 0, tiled=True)

    x_in = received[:, :group, :].reshape(n_src, rk, cap, width)
    info = received[:, group, :].astype(F32)
    span_in = info[:, :nch].astype(jnp.int32)
    count_in = info[:, nch : nch + rk]
    dst_in = info[:, nch + rk : nch + rk + group].astype(jnp.int32)
    mapped = jnp.einsum(
        "pkcd,kde->pkce", x_in, rel_ops, preferred_element_type=F32
    ).astype(BF16)
    mapped_back = lax.all_to_all(mapped, "src", 0, 0, tiled=True)

    z_in = mapped.reshape(n_src, group, width)
    y_in = dst_emb[dst_in.reshape(-1)].reshape(n_src, group, width)
    negs_in = every_dst[span_in].reshape(n_src, nch * part, width)
    lane = jnp.arange(cap, dtype=F32)
    live_in = (lane[None, None, :] < count_in[:, :, None]).astype(F32).reshape(n_src, group)
    g_neg, g_pos = softmax_grads(z_in, y_in, negs_in, live_in)
    upstream = (
        g_pos[..., None] * y_in.astype(F32)
        + jnp.einsum("pmn,pnd->pmd", g_neg, negs_in, preferred_element_type=F32)
    ).astype(BF16)
    upstream = upstream.reshape(n_src, rk, cap, width)
    grad_rel = jnp.einsum(
        "pkcd,pkce->kde", x_in, upstream, preferred_element_type=F32
    ).astype(BF16)
    back_rows = jnp.einsum(
        "pkce,kde->pkcd", upstream, rel_ops, preferred_element_type=F32
    ).astype(BF16)
    back_rows = lax.all_to_all(back_rows, "src", 0, 0, tiled=True)

    src_local = jax.ops.segment_sum(
        back_rows.reshape(slots, width).astype(F32), ids_src, num_segments=part
    )
    grad_src = butterfly_sum(src_local, "dst", axis_bits(n_dst)).astype(BF16)

    z_b = mapped_back.reshape(slots, width)
    y_b = dst_emb[ids_dst]
    negs = every_dst[spans].reshape(nch * part, width)
    slot_lane = jnp.arange(slots, dtype=jnp.int32) % cap
    live = (
        slot_lane < jnp.repeat(counts, cap, total_repeat_length=slots)
    ).astype(F32)
    g_neg_b, g_pos_b = softmax_grads(z_b, y_b, negs, live)
    dst_local = jax.ops.segment_sum(
        g_pos_b[:, None] * z_b.astype(F32), ids_dst, num_segments=part
    )
    span_grad = jnp.einsum("bn,bd->nd", g_neg_b, z_b, preferred_element_type=F32)
    span_sum = butterfly_sum(span_grad, "dst", axis_bits(n_dst))
    for index in range(nch):
        piece = span_sum[index * part : (index + 1) * part]
        dst_local = dst_local + jnp.where(spans[index] == own_dst, piece, 0.0)
    grad_dst = butterfly_sum(dst_local, "src", axis_bits(n_src)).astype(BF16)
    return (grad_rel, grad_src, grad_dst)


def solution(mesh):
    placed = (
        P(("src", "dst"), None, None),
        P("src", None),
        P("dst", None),
        P("src", "dst", None),
        P("src", "dst", None),
        P("src", "dst", None),
        P("src", None),
    )
    return jax.shard_map(
        body,
        mesh=mesh,
        in_specs=placed,
        out_specs=(P(("src", "dst"), None, None), P("src", None), P("dst", None)),
        check_vma=False,
    )
```

time: 1060 us -> 499 us (0.47)
  blocking collectives: 356 us -> 0 us
  waiting for transfers between devices: 552 us -> 225 us
  starting transfers between devices: 18.1 us -> 96.3 us
  local copies, waits for them, and re-layouts: 35.9 us -> 64 us
  matrix products: 9.77 us -> 21.9 us
    psum x2 -> x0, waiting for transfers between devices: 552 us -> none  [the longest x1 287 us: body(): lax.psum(span_grad.astype(jnp.bfloat16), 'dst').astype(jnp.float32)]
    psum x2 -> x0, blocking collectives: 242 us -> none  [the longest x1 143 us: body(): grad_src = lax.psum(src_local, 'dst').astype(jnp.bfloat16)]
    all_to_all x2 -> x0, blocking collectives: 114 us -> none  [the longest x1 67 us: body(): lax.all_to_all(inputs, 'src', split_axis=0, concat_axis=0, tiled=True)]
    ppermute x0 -> x14, waiting for transfers between devices: none -> 109 us  [butterfly_sum(): other = lax.ppermute(low, axis, [(i, i ^ bit) for i in range(n)])]
    all_to_all x2 -> x3, waiting for transfers between devices: 0.01 us -> 107 us  [the longest x1 62.7 us: body(): received = lax.all_to_all(payload, 'src', 0, 0, tiled=True)]
    ppermute x0 -> x14, starting transfers between devices: none -> 54 us  [butterfly_sum(): other = lax.ppermute(low, axis, [(i, i ^ bit) for i in range(n)])]
    mul x2, other arithmetic: 0.03 us -> 37.3 us  [softmax_grads(): g_pos = (exp_pos / denom - 1.0) * live]
    gather x5 -> x7, other arithmetic: 40.7 us -> 5.83 us  [the longest x2 5.81 us: body(): jnp.repeat(counts, cap, total_repeat_length=slots)]
  transfers between devices with their start and end apart: 4 -> 18, of which waited for: 2 -> 12; matrix products, arithmetic and copies ran while one was open for 7% -> 15% of each run, Pallas kernels for 0% -> 0%
where the time goes in v1:
time: 499 us; the launch traced here: 497 us
  waiting for transfers between devices  225 us (45%)
  starting transfers between devices  96.3 us (19%)
  other arithmetic  72.7 us (15%)
  local copies, waits for them, and re-layouts  64 us (13%)
  matrix products  21.9 us (4%)
  between operations  16.6 us (3%)
    ppermute x14, waiting for transfers between devices, butterfly_sum(): other = lax.ppermute(low, axis, [(i, i ^ bit) for i in range(n)])  109 us
    all_to_all x1, waiting for transfers between devices, body(): received = lax.all_to_all(payload, 'src', 0, 0, tiled=True)  62.7 us
    ppermute x14, starting transfers between devices, butterfly_sum(): other = lax.ppermute(low, axis, [(i, i ^ bit) for i in range(n)])  54 us
    all_to_all x1, waiting for transfers between devices, body(): mapped_back = lax.all_to_all(mapped, 'src', 0, 0, tiled=True)  44.5 us
    mul x2, other arithmetic, softmax_grads(): g_pos = (exp_pos / denom - 1.0) * live  37.3 us
    all_to_all x1, starting transfers between devices, body(): received = lax.all_to_all(payload, 'src', 0, 0, tiled=True)  18.2 us
    gather x2, local copies, waits for them, and re-layouts, body(): negs_in = every_dst[span_in].reshape(n_src, nch * part, width)  14.5 us
    all_to_all x1, starting transfers between devices, body(): mapped_back = lax.all_to_all(mapped, 'src', 0, 0, tiled=True)  13.2 us
  transfers between devices with their start and end apart: 18, of which 12 were waited for; matrix products, arithmetic and copies ran while one was open for 15% of the time, Pallas kernels for 0%

profile of v1, /device:TPU:1, one launch (start us, length us, event | category | flops | bytes accessed | tf_op | source)
XLA Modules:
  0.0 496.6 jit_solution(3722727539848356520)
XLA Ops:
  12.0 5.1 %gather_fusion = bf16[1024,400]{1,0:T(8,128)(2,1)} fusion(bf16[256,400]{1,0:T(8,128)(2,1)S(1)} %copy.78, s32[1024]{0:T(1024)S(1)} %broadcast_clamp_fusion.2), kind=kCustom, calls=%fused_computation | custom fusion | bytes 1642496 | tf_op jit(solution)/shard_map/gather | solution.py:62
  19.6 18.2 %all-to-all-start = ((bf16[16,65,400]{2,1,0:T(8,128)(2,1)}), bf16[16,65,400]{2,1,0:T(8,128)(2,1)}, u32[]{:S(2)}, u32[]{:S(2)}) async-start(bf16[16,65,400]{2,1,0:T(8,128)(2,1)} %pad_maximum_fusion), calls=%async_computation | async-start | bytes 2359296 | tf_op jit(solution)/shard_map/all_to_all | solution.py:64
  38.0 62.7 %all-to-all-done = bf16[16,65,400]{2,1,0:T(8,128)(2,1)} async-done(((bf16[16,65,400]{2,1,0:T(8,128)(2,1)}), bf16[16,65,400]{2,1,0:T(8,128)(2,1)}, u32[]{:S(2)}, u32[]{:S(2)}) %all-to-all-start) | async-done | bytes 832032 | tf_op jit(solution)/shard_map/all_to_all | solution.py:64
  101.7 4.0 gather_fusion.1
  110.2 13.2 %all-to-all-start.2 = ((bf16[16,4,16,400]{3,2,1,0:T(8,128)(2,1)}), bf16[16,4,16,400]{3,2,1,0:T(8,128)(2,1)S(1)}, u32[]{:S(2)}, u32[]{:S(2)}) async-start(bf16[16,4,16,400]{3,2,1,0:T(8,128)(2,1)} %copy.84), calls=%async_computation.2 | async-start | bytes 2097152 | tf_op jit(solution)/shard_map/all_to_all | solution.py:74
  124.1 5.1 %gather_fusion.4 = bf16[1024,400]{1,0:T(8,128)(2,1)} fusion(bf16[256,400]{1,0:T(8,128)(2,1)S(1)} %copy.81, s32[1024]{0:T(1024)S(1)} %broadcast_clamp_fusion), kind=kCustom, calls=%fused_computation.4 | custom fusion | bytes 1642496 | tf_op jit(solution)/shard_map/gather | solution.py:101
  132.2 4.3 compare_select_fusion.5
  138.4 44.5 %all-to-all-done.2 = bf16[16,4,16,400]{3,2,1,0:T(8,128)(2,1)S(1)} async-done(((bf16[16,4,16,400]{3,2,1,0:T(8,128)(2,1)}), bf16[16,4,16,400]{3,2,1,0:T(8,128)(2,1)S(1)}, u32[]{:S(2)}, u32[]{:S(2)}) %all-to-all-start.2) | async-done | bytes 819232 | tf_op jit(solution)/shard_map/all_to_all | solution.py:74
  184.6 8.0 %all-gather.3.cloned.1.call-done = bf16[8192,400]{0,1:T(8,128)(2,1)} async-done(((bf16[256,400]{0,1:T(8,128)(2,1)}), bf16[8192,400]{0,1:T(8,128)(2,1)}) %all-gather.3.cloned.1.call-update) | async-done | bytes 6553616 | tf_op jit(solution)/shard_map/all_gather | solution.py:51
  192.6 6.0 %copy.129 = bf16[50,32,8,256]{3,2,0,1:T(8,128)(2,1)} copy(bf16[50,32,8,256]{3,2,1,0:T(8,128)(2,1)} %bitcast.155) | data formatting | bytes 13107200 | tf_op jit(solution)/shard_map/all_gather | solution.py:51
  202.1 6.6 %gather_fusion.2 = bf16[32,256,400]{1,2,0:T(8,128)(2,1)} fusion(bf16[32,256,400]{1,2,0:T(8,128)(2,1)} %bitcast.148, s32[1024]{0:T(1024)S(1)} %pad_clamp_fusion.1), kind=kCustom, calls=%fused_computation.2 | custom fusion | bytes 13107328 | tf_op jit(solution)/shard_map/gather | solution.py:78
  208.6 7.9 %copy.86 = bf16[32,256,400]{1,0,2:T(8,128)(2,1)} copy(bf16[32,256,400]{1,2,0:T(8,128)(2,1)} %gather_fusion.2) | data formatting | bytes 13107200 | tf_op jit(solution)/shard_map/gather | solution.py:78
  216.5 10.7 %reshape.399 = bf16[16,512,400]{1,0,2:T(8,128)(2,1)} reshape(bf16[32,256,400]{1,0,2:T(8,128)(2,1)} %copy.86) | data formatting | bytes 13107200 | tf_op jit(solution)/shard_map/reshape | solution.py:78
  229.1 37.3 %add_select_fusion.2 = (f32[1024]{0:T(1024)S(1)}, pred[1024]{0:T(1024)(128)(4,1)S(1)}) fusion(f32[1024]{0:T(1024)S(1)} %fusion.12, f32[1024]{0:T(1024)S(1)} %reduce_sum.44, f32[1024]{0:T(1024)S(1)} %max.27, pred[1024]{0:T(1024)(128)(4,1)} %get-tuple-element.83, pred[1024]{0:T(1024)(128)(4,1)} %get-tuple-element.82, pred[1024]{0:T(1024)(128)(4,1)} %get-tuple-element.81, ...), kind=kLoop, calls=%fused_computation.149 | loop fusion | flops 79872 | bytes 84228 | tf_op jit(solution)/shard_map/mul | solution.py:31
  269.5 7.1 %fusion.51 = (f32[16,64]{1,0:T(8,128)S(1)}, f32[16,64,512]{2,1,0:T(8,128)S(1)}) fusion(bf16[16,64,400]{2,1,0:T(8,128)(2,1)S(1)} %bitcast.154, bf16[16,512,400]{1,0,2:T(8,128)(2,1)S(1)} %copy-done.1), kind=kOutput, calls=%fused_computation.171 | convolution fusion | flops 419953664 | bytes 9474048 | tf_op jit(solution)/shard_map/...md,...nd->...mn/dot_general | solution.py:24
  278.2 8.4 %add_convert_fusion = bf16[16,64,400]{2,1,0:T(8,128)(2,1)S(1)} fusion(f32[16,64,400]{2,1,0:T(8,128)S(1)} %bitcast.150, bf16[16,512,400]{1,0,2:T(8,128)(2,1)S(1)} %copy-done.1, f32[16,64,512]{2,1,0:T(8,128)S(1)} %get-tuple-element.159, f32[16,64]{1,0:T(8,128)S(1)} %convert_divide_fusion, f32[16,64]{1,0:T(8,128)S(1)} %get-tuple-element.88, f32[16,64]{1,0:T(8,128)S(1)} %max.26), kind=kOutput, calls=%fused_computation.24 | convolution fusion | flops 422232064 | bytes 11120640 | tf_op jit(solution)/shard_map/pmn,pnd->pmd/dot_general | solution.py:84
  289.5 10.7 %all-to-all-start.1 = ((bf16[16,4,16,400]{3,2,1,0:T(8,128)(2,1)}), bf16[16,4,16,400]{3,2,1,0:T(8,128)(2,1)}, u32[]{:S(2)}, u32[]{:S(2)}) async-start(bf16[16,4,16,400]{3,2,1,0:T(8,128)(2,1)} %copy.90), calls=%async_computation.1 | async-start | bytes 2097152 | tf_op jit(solution)/shard_map/all_to_all | solution.py:93
  302.2 10.6 %collective-permute-done.6 = bf16[512,400]{0,1:T(8,128)(2,1)S(1)} collective-permute-done((bf16[512,400]{0,1:T(8,128)(2,1)S(1)}, bf16[512,400]{0,1:T(8,128)(2,1)S(1)}, u32[]{:S(2)}, u32[]{:S(2)}) %collective-permute-start.6) | collective-permute-done | bytes 409632 | tf_op jit(solution)/shard_map/ppermute | solution.py:14
  315.4 10.8 %collective-permute-done.7 = bf16[512,400]{0,1:T(8,128)(2,1)S(1)} collective-permute-done((bf16[512,400]{0,1:T(8,128)(2,1)S(1)}, bf16[512,400]{0,1:T(8,128)(2,1)S(1)}, u32[]{:S(2)}, u32[]{:S(2)}) %collective-permute-start.7) | collective-permute-done | bytes 409632 | tf_op jit(solution)/shard_map/ppermute | solution.py:14
  326.3 5.2 %collective-permute-start.8 = (bf16[512,400]{0,1:T(8,128)(2,1)S(1)}, bf16[512,400]{0,1:T(8,128)(2,1)S(1)}, u32[]{:S(2)}, u32[]{:S(2)}) collective-permute-start(bf16[512,400]{0,1:T(8,128)(2,1)S(1)} %add_convert_fusion.2), channel_id=1, source_target_pairs={{0,8},{1,9},{2,10},{3,11},{4,12},{5,13},{6,14},{7,15},{8,0},{9,1},... | collective-permute-start | bytes 1228808 | tf_op jit(solution)/shard_map/ppermute | solution.py:14
  333.4 20.9 %collective-permute-done.8 = bf16[512,400]{0,1:T(8,128)(2,1)S(1)} collective-permute-done((bf16[512,400]{0,1:T(8,128)(2,1)S(1)}, bf16[512,400]{0,1:T(8,128)(2,1)S(1)}, u32[]{:S(2)}, u32[]{:S(2)}) %collective-permute-start.8) | collective-permute-done | bytes 409632 | tf_op jit(solution)/shard_map/ppermute | solution.py:14
  354.4 7.2 %collective-permute-start.9 = (bf16[512,400]{0,1:T(8,128)(2,1)S(1)}, bf16[512,400]{0,1:T(8,128)(2,1)S(1)}, u32[]{:S(2)}, u32[]{:S(2)}) collective-permute-start(bf16[512,400]{0,1:T(8,128)(2,1)S(1)} %add_convert_fusion.1), channel_id=1, source_target_pairs={{0,16},{1,17},{2,18},{3,19},{4,20},{5,21},{6,22},{7,23},{8,24},{9,... | collective-permute-start | bytes 1228808 | tf_op jit(solution)/shard_map/ppermute | solution.py:14
  365.0 14.4 %collective-permute-done.9 = bf16[512,400]{0,1:T(8,128)(2,1)S(1)} collective-permute-done((bf16[512,400]{0,1:T(8,128)(2,1)S(1)}, bf16[512,400]{0,1:T(8,128)(2,1)S(1)}, u32[]{:S(2)}, u32[]{:S(2)}) %collective-permute-start.9) | collective-permute-done | bytes 409632 | tf_op jit(solution)/shard_map/ppermute | solution.py:14
  380.4 7.3 %scatter_custom_fusion = f32[256,400]{1,0:T(8,128)S(1)} fusion(s32[1024]{0:T(1024)} %bitcast.174, bf16[1024,400]{1,0:T(8,128)(2,1)} %bitcast.97, f32[]{:T(128)} %constant.119.clone.1), kind=kCustom, calls=%fused_computation.15 | custom fusion | flops 819200 | bytes 1458688 | tf_op jit(solution)/shard_map/scatter-add | solution.py:95
  393.3 7.6 %scatter_custom_fusion.1 = f32[256,400]{1,0:T(8,128)S(1)} fusion(f32[256,400]{1,0:T(8,128)S(1)} %copy.98, s32[1024]{0:T(1024)S(1)} %bitcast.170, bf16[1024,400]{1,0:T(8,128)(2,1)S(1)} %bitcast.153, f32[1024]{0:T(1024)S(1)} %get-tuple-element.84), kind=kCustom, calls=%fused_computation.19 | custom fusion | flops 1228800 | bytes 1462272 | tf_op jit(solution)/shard_map/scatter-add | solution.py:108
  407.2 3.5 collective-permute-done.10
  410.8 4.6 collective-permute-start.11
  421.2 6.7 %collective-permute-start.12 = (bf16[256,400]{1,0:T(8,128)(2,1)S(1)}, bf16[256,400]{1,0:T(8,128)(2,1)S(1)}, u32[]{:S(2)}, u32[]{:S(2)}) collective-permute-start(bf16[256,400]{1,0:T(8,128)(2,1)S(1)} %add_convert_fusion.7), channel_id=1, source_target_pairs={{0,128},{32,160},{64,192},{96,224},{128,0},{160,32},{192,64},{224,... | collective-permute-start | bytes 614408 | tf_op jit(solution)/shard_map/ppermute | solution.py:14
  429.9 21.2 %collective-permute-done.12 = bf16[256,400]{1,0:T(8,128)(2,1)S(1)} collective-permute-done((bf16[256,400]{1,0:T(8,128)(2,1)S(1)}, bf16[256,400]{1,0:T(8,128)(2,1)S(1)}, u32[]{:S(2)}, u32[]{:S(2)}) %collective-permute-start.12) | collective-permute-done | bytes 204832 | tf_op jit(solution)/shard_map/ppermute | solution.py:14
  451.2 9.1 %collective-permute-start.13 = (bf16[256,400]{1,0:T(8,128)(2,1)S(1)}, bf16[256,400]{1,0:T(8,128)(2,1)S(1)}, u32[]{:S(2)}, u32[]{:S(2)}) collective-permute-start(bf16[256,400]{1,0:T(8,128)(2,1)S(1)} %add_convert_fusion.6), channel_id=1, source_target_pairs={{0,256},{32,288},{64,320},{96,352},{128,384},{160,416},{192,448},{... | collective-permute-start | bytes 614408 | tf_op jit(solution)/shard_map/ppermute | solution.py:14
  462.3 19.1 %collective-permute-done.13 = bf16[256,400]{1,0:T(8,128)(2,1)S(1)} collective-permute-done((bf16[256,400]{1,0:T(8,128)(2,1)S(1)}, bf16[256,400]{1,0:T(8,128)(2,1)S(1)}, u32[]{:S(2)}, u32[]{:S(2)}) %collective-permute-start.13) | collective-permute-done | bytes 204832 | tf_op jit(solution)/shard_map/ppermute | solution.py:14
  482.3 6.6 %collective-permute-done.4 = bf16[256,400]{1,0:T(8,128)(2,1)S(1)} collective-permute-done((bf16[256,400]{1,0:T(8,128)(2,1)S(1)}, bf16[256,400]{1,0:T(8,128)(2,1)S(1)}, u32[]{:S(2)}, u32[]{:S(2)}) %collective-permute-start.4) | collective-permute-done | bytes 204832 | tf_op jit(solution)/shard_map/ppermute | solution.py:14
  (208 shorter events, 65.6 us)
Async XLA Ops:
  7.2 101.0 %copy-start = (bf16[4,400,400]{2,1,0:T(8,128)(2,1)S(1)}, bf16[4,400,400]{2,1,0:T(8,128)(2,1)}, u32[]{:S(2)}) copy-start(bf16[4,400,400]{2,1,0:T(8,128)(2,1)} %param.9) | copy-start | bytes 3840004
  7.2 185.4 %all-gather.3.cloned.1.call-start = ((), (), s32[]{:S(2)}) async-start(), calls=%async_computation.3 | async-start | bytes 6758400 | tf_op jit(solution)/shard_map/all_gather | solution.py:51
  17.1 20.7 %copy-start.9 = (bf16[256,400]{0,1:T(8,128)(2,1)S(1)}, bf16[256,400]{0,1:T(8,128)(2,1)}, u32[]{:S(2)}) copy-start(bf16[256,400]{0,1:T(8,128)(2,1)} %param.11) | copy-start | bytes 614404
  19.6 81.1 %all-to-all-start = ((bf16[16,65,400]{2,1,0:T(8,128)(2,1)}), bf16[16,65,400]{2,1,0:T(8,128)(2,1)}, u32[]{:S(2)}, u32[]{:S(2)}) async-start(bf16[16,65,400]{2,1,0:T(8,128)(2,1)} %pad_maximum_fusion), calls=%async_computation | async-start | bytes 2359296 | tf_op jit(solution)/shard_map/all_to_all | solution.py:64
  106.0 2.9 copy-start.2
  109.1 14.9 %copy-start.11 = (s32[1,1,1024]{2,1,0:T(1,128)S(1)}, s32[1,1,1024]{2,1,0:T(1,128)}, u32[]{:S(2)}) copy-start(s32[1,1,1024]{2,1,0:T(1,128)} %param.13) | copy-start | bytes 12292
  110.2 72.7 %all-to-all-start.2 = ((bf16[16,4,16,400]{3,2,1,0:T(8,128)(2,1)}), bf16[16,4,16,400]{3,2,1,0:T(8,128)(2,1)S(1)}, u32[]{:S(2)}, u32[]{:S(2)}) async-start(bf16[16,4,16,400]{3,2,1,0:T(8,128)(2,1)} %copy.84), calls=%async_computation.2 | async-start | bytes 2097152 | tf_op jit(solution)/shard_map/all_to_all | solution.py:74
  124.1 5.1 %copy-start.52 = (s32[1,2]{1,0:T(1,128)S(1)}, s32[1,2]{1,0:T(1,128)}, u32[]{:S(2)}) copy-start(s32[1,2]{1,0:T(1,128)} %param.15) | copy-start | bytes 28
  124.1 5.1 %copy-start.7 = (s32[1,1,64]{2,1,0:T(1,128)S(1)}, s32[1,1,64]{2,1,0:T(1,128)}, u32[]{:S(2)}) copy-start(s32[1,1,64]{2,1,0:T(1,128)} %param.14) | copy-start | bytes 772
  124.1 8.0 %copy-start.10 = (s32[8,128]{1,0:T(8,128)S(1)}, s32[8,128]{1,0:T(8,128)}, u32[]{:S(2)}) copy-start(s32[8,128]{1,0:T(8,128)} %constant.127.clone.1) | copy-start | bytes 12292
  129.2 3.0 copy-start.51
  227.2 1.5 copy-start.16
  227.5 41.9 %copy-start.1 = (bf16[16,512,400]{1,0,2:T(8,128)(2,1)S(1)}, bf16[16,512,400]{1,0,2:T(8,128)(2,1)}, u32[]{:S(2)}) copy-start(bf16[16,512,400]{1,0,2:T(8,128)(2,1)} %reshape.399) | copy-start | bytes 19660804
  228.7 40.8 %copy-start.4 = (bf16[16,4,16,400]{3,2,1,0:T(8,128)(2,1)S(1)}, bf16[16,4,16,400]{3,2,1,0:T(8,128)(2,1)}, u32[]{:S(2)}) copy-start(bf16[16,4,16,400]{3,2,1,0:T(8,128)(2,1)} %copy.84) | copy-start | bytes 2457604
  267.1 33.1 %collective-permute-start.5 = (bf16[512,400]{0,1:T(8,128)(2,1)S(1)}, bf16[512,400]{0,1:T(8,128)(2,1)S(1)}, u32[]{:S(2)}, u32[]{:S(2)}) collective-permute-start(bf16[512,400]{0,1:T(8,128)(2,1)S(1)} %convolution_convert_fusion), channel_id=1, source_target_pairs={{0,1},{1,0},{2,3},{3,2},{4,5},{5,4},{6,7},{7,6},{8,9},{9,8},{10,11... | collective-permute-start | bytes 1228808 | tf_op jit(solution)/shard_map/ppermute | solution.py:14
  276.6 1.6 copy-start.3
  289.5 90.9 %all-to-all-start.1 = ((bf16[16,4,16,400]{3,2,1,0:T(8,128)(2,1)}), bf16[16,4,16,400]{3,2,1,0:T(8,128)(2,1)}, u32[]{:S(2)}, u32[]{:S(2)}) async-start(bf16[16,4,16,400]{3,2,1,0:T(8,128)(2,1)} %copy.90), calls=%async_computation.1 | async-start | bytes 2097152 | tf_op jit(solution)/shard_map/all_to_all | solution.py:93
  300.2 31.3 %copy-start.53 = (s32[1,2]{1,0:T(1,128)S(1)}, s32[1,2]{1,0:T(1,128)}, u32[]{:S(2)}) copy-start(s32[1,2]{1,0:T(1,128)} %param.15) | copy-start | bytes 28
  300.3 12.5 %collective-permute-start.6 = (bf16[512,400]{0,1:T(8,128)(2,1)S(1)}, bf16[512,400]{0,1:T(8,128)(2,1)S(1)}, u32[]{:S(2)}, u32[]{:S(2)}) collective-permute-start(bf16[512,400]{0,1:T(8,128)(2,1)S(1)} %add_convert_fusion.4), channel_id=1, source_target_pairs={{0,2},{1,3},{2,0},{3,1},{4,6},{5,7},{6,4},{7,5},{8,10},{9,11},{10,... | collective-permute-start | bytes 1228808 | tf_op jit(solution)/shard_map/ppermute | solution.py:14
  312.9 13.3 %collective-permute-start.7 = (bf16[512,400]{0,1:T(8,128)(2,1)S(1)}, bf16[512,400]{0,1:T(8,128)(2,1)S(1)}, u32[]{:S(2)}, u32[]{:S(2)}) collective-permute-start(bf16[512,400]{0,1:T(8,128)(2,1)S(1)} %add_convert_fusion.3), channel_id=1, source_target_pairs={{0,4},{1,5},{2,6},{3,7},{4,0},{5,1},{6,2},{7,3},{8,12},{9,13},{10,... | collective-permute-start | bytes 1228808 | tf_op jit(solution)/shard_map/ppermute | solution.py:14
  326.3 28.0 %collective-permute-start.8 = (bf16[512,400]{0,1:T(8,128)(2,1)S(1)}, bf16[512,400]{0,1:T(8,128)(2,1)S(1)}, u32[]{:S(2)}, u32[]{:S(2)}) collective-permute-start(bf16[512,400]{0,1:T(8,128)(2,1)S(1)} %add_convert_fusion.2), channel_id=1, source_target_pairs={{0,8},{1,9},{2,10},{3,11},{4,12},{5,13},{6,14},{7,15},{8,0},{9,1},... | collective-permute-start | bytes 1228808 | tf_op jit(solution)/shard_map/ppermute | solution.py:14
  354.4 24.9 %collective-permute-start.9 = (bf16[512,400]{0,1:T(8,128)(2,1)S(1)}, bf16[512,400]{0,1:T(8,128)(2,1)S(1)}, u32[]{:S(2)}, u32[]{:S(2)}) collective-permute-start(bf16[512,400]{0,1:T(8,128)(2,1)S(1)} %add_convert_fusion.1), channel_id=1, source_target_pairs={{0,16},{1,17},{2,18},{3,19},{4,20},{5,21},{6,22},{7,23},{8,24},{9,... | collective-permute-start | bytes 1228808 | tf_op jit(solution)/shard_map/ppermute | solution.py:14
  387.7 2.4 copy-start.5
  387.8 16.3 %collective-permute-start = (bf16[256,400]{1,0:T(8,128)(2,1)S(1)}, bf16[256,400]{1,0:T(8,128)(2,1)}, u32[]{:S(2)}, u32[]{:S(2)}) collective-permute-start(bf16[256,400]{1,0:T(8,128)(2,1)S(1)} %convert_element_type.243), channel_id=1, source_target_pairs={{0,1},{1,0},{2,3},{3,2},{4,5},{5,4},{6,7},{7,6},{8,9},{9,8},{10,11... | collective-permute-start | bytes 614408 | tf_op jit(solution)/shard_map/ppermute | solution.py:14
  401.0 9.7 %collective-permute-start.10 = (bf16[256,400]{1,0:T(8,128)(2,1)S(1)}, bf16[256,400]{1,0:T(8,128)(2,1)S(1)}, u32[]{:S(2)}, u32[]{:S(2)}) collective-permute-start(bf16[256,400]{1,0:T(8,128)(2,1)S(1)} %convert_element_type.280), channel_id=1, source_target_pairs={{0,32},{32,0},{64,96},{96,64},{128,160},{160,128},{192,224},{224,1... | collective-permute-start | bytes 614408 | tf_op jit(solution)/shard_map/ppermute | solution.py:14
  405.3 10.1 %collective-permute-start.1 = (bf16[256,400]{1,0:T(8,128)(2,1)S(1)}, bf16[256,400]{1,0:T(8,128)(2,1)S(1)}, u32[]{:S(2)}, u32[]{:S(2)}) collective-permute-start(bf16[256,400]{1,0:T(8,128)(2,1)S(1)} %add_convert_fusion.13), channel_id=1, source_target_pairs={{0,2},{1,3},{2,0},{3,1},{4,6},{5,7},{6,4},{7,5},{8,10},{9,11},{10,... | collective-permute-start | bytes 614408 | tf_op jit(solution)/shard_map/ppermute | solution.py:14
  410.8 10.4 %collective-permute-start.11 = (bf16[256,400]{1,0:T(8,128)(2,1)S(1)}, bf16[256,400]{1,0:T(8,128)(2,1)S(1)}, u32[]{:S(2)}, u32[]{:S(2)}) collective-permute-start(bf16[256,400]{1,0:T(8,128)(2,1)S(1)} %add_convert_fusion.8), channel_id=1, source_target_pairs={{0,64},{32,96},{64,0},{96,32},{128,192},{160,224},{192,128},{224,1... | collective-permute-start | bytes 614408 | tf_op jit(solution)/shard_map/ppermute | solution.py:14
  415.4 12.4 %collective-permute-start.2 = (bf16[256,400]{1,0:T(8,128)(2,1)S(1)}, bf16[256,400]{1,0:T(8,128)(2,1)S(1)}, u32[]{:S(2)}, u32[]{:S(2)}) collective-permute-start(bf16[256,400]{1,0:T(8,128)(2,1)S(1)} %add_convert_fusion.12), channel_id=1, source_target_pairs={{0,4},{1,5},{2,6},{3,7},{4,0},{5,1},{6,2},{7,3},{8,12},{9,13},{10,... | collective-permute-start | bytes 614408 | tf_op jit(solution)/shard_map/ppermute | solution.py:14
  421.2 29.9 %collective-permute-start.12 = (bf16[256,400]{1,0:T(8,128)(2,1)S(1)}, bf16[256,400]{1,0:T(8,128)(2,1)S(1)}, u32[]{:S(2)}, u32[]{:S(2)}) collective-permute-start(bf16[256,400]{1,0:T(8,128)(2,1)S(1)} %add_convert_fusion.7), channel_id=1, source_target_pairs={{0,128},{32,160},{64,192},{96,224},{128,0},{160,32},{192,64},{224,... | collective-permute-start | bytes 614408 | tf_op jit(solution)/shard_map/ppermute | solution.py:14
  428.0 32.3 %collective-permute-start.3 = (bf16[256,400]{1,0:T(8,128)(2,1)S(1)}, bf16[256,400]{1,0:T(8,128)(2,1)S(1)}, u32[]{:S(2)}, u32[]{:S(2)}) collective-permute-start(bf16[256,400]{1,0:T(8,128)(2,1)S(1)} %add_convert_fusion.11), channel_id=1, source_target_pairs={{0,8},{1,9},{2,10},{3,11},{4,12},{5,13},{6,14},{7,15},{8,0},{9,1},... | collective-permute-start | bytes 614408 | tf_op jit(solution)/shard_map/ppermute | solution.py:14
  451.2 30.2 %collective-permute-start.13 = (bf16[256,400]{1,0:T(8,128)(2,1)S(1)}, bf16[256,400]{1,0:T(8,128)(2,1)S(1)}, u32[]{:S(2)}, u32[]{:S(2)}) collective-permute-start(bf16[256,400]{1,0:T(8,128)(2,1)S(1)} %add_convert_fusion.6), channel_id=1, source_target_pairs={{0,256},{32,288},{64,320},{96,352},{128,384},{160,416},{192,448},{... | collective-permute-start | bytes 614408 | tf_op jit(solution)/shard_map/ppermute | solution.py:14
  460.4 28.5 %collective-permute-start.4 = (bf16[256,400]{1,0:T(8,128)(2,1)S(1)}, bf16[256,400]{1,0:T(8,128)(2,1)S(1)}, u32[]{:S(2)}, u32[]{:S(2)}) collective-permute-start(bf16[256,400]{1,0:T(8,128)(2,1)S(1)} %add_convert_fusion.10), channel_id=1, source_target_pairs={{0,16},{1,17},{2,18},{3,19},{4,20},{5,21},{6,22},{7,23},{8,24},{9,... | collective-permute-start | bytes 614408 | tf_op jit(solution)/shard_map/ppermute | solution.py:14
  (40 other events, 59.3 us)
Sparse Core Ops, SparseCore 0:
  10.0 182.4 all-gather.2

commit v2 on v1

--- a/solution.py
+++ b/solution.py
@@ -18,6 +18,42 @@
 
 def axis_bits(n):
     return [1 << b for b in range(n.bit_length() - 1)]
+
+
+def group_round(x, axis, stride, size):
+    n = lax.axis_size(axis)
+    me = lax.axis_index(axis)
+    member = (me // stride) % size
+    low = x.astype(BF16)
+    got = [low]
+    for shift in range(1, size):
+        perm = []
+        for i in range(n):
+            m = (i // stride) % size
+            perm.append((i, i + (((m + shift) % size) - m) * stride))
+        got.append(lax.ppermute(low, axis, perm))
+    stacked = jnp.stack(got)
+    order = (member - jnp.arange(size)) % size
+    ordered = stacked[order].astype(F32)
+    total = ordered[0]
+    for j in range(1, size):
+        total = total + ordered[j]
+    return total
+
+
+def sub_axes(n):
+    shapes = {32: ((1, 2), (2, 4), (8, 4)), 16: ((1, 4), (4, 4))}
+    return shapes.get(n)
+
+
+def axis_sum(x, axis):
+    n = lax.axis_size(axis)
+    parts = sub_axes(n)
+    if parts is None:
+        return butterfly_sum(x, axis, axis_bits(n))
+    for stride, size in parts:
+        x = group_round(x, axis, stride, size)
+    return x
 
 
 def softmax_grads(z, y, negs, live):
@@ -95,7 +131,6 @@
     src_local = jax.ops.segment_sum(
         back_rows.reshape(slots, width).astype(F32), ids_src, num_segments=part
     )
-    grad_src = butterfly_sum(src_local, "dst", axis_bits(n_dst)).astype(BF16)
 
     z_b = mapped_back.reshape(slots, width)
     y_b = dst_emb[ids_dst]
@@ -109,11 +144,13 @@
         g_pos_b[:, None] * z_b.astype(F32), ids_dst, num_segments=part
     )
     span_grad = jnp.einsum("bn,bd->nd", g_neg_b, z_b, preferred_element_type=F32)
-    span_sum = butterfly_sum(span_grad, "dst", axis_bits(n_dst))
+    joint = axis_sum(jnp.concatenate([src_local, span_grad], 0), "dst")
+    grad_src = joint[:part].astype(BF16)
+    span_sum = joint[part:]
     for index in range(nch):
         piece = span_sum[index * part : (index + 1) * part]
         dst_local = dst_local + jnp.where(spans[index] == own_dst, piece, 0.0)
-    grad_dst = butterfly_sum(dst_local, "src", axis_bits(n_src)).astype(BF16)
+    grad_dst = axis_sum(dst_local, "src").astype(BF16)
     return (grad_rel, grad_src, grad_dst)
 
 

time: 499 us -> 536 us (1.074)
  the two profiles are of different devices: /device:TPU:1 before, /device:TPU:4 now
where the time goes in v2:
time: 536 us; the launch traced here: 528 us
  waiting for transfers between devices  241 us (45%)
  starting transfers between devices  92.9 us (17%)
  other arithmetic  78.6 us (15%)
  local copies, waits for them, and re-layouts  75 us (14%)
  matrix products  23.8 us (4%)
  between operations  16.4 us (3%)
    ppermute x13, waiting for transfers between devices, group_round(): got.append(lax.ppermute(low, axis, perm))  110 us
    all_gather x1, waiting for transfers between devices, body(): every_dst = lax.all_gather(dst_emb, 'dst', tiled=False)  71 us
    all_to_all x1, waiting for transfers between devices, body(): received = lax.all_to_all(payload, 'src', 0, 0, tiled=True)  59.2 us
    ppermute x13, starting transfers between devices, group_round(): got.append(lax.ppermute(low, axis, perm))  52.5 us
    mul x2, other arithmetic, softmax_grads(): g_pos = (exp_pos / denom - 1.0) * live  35.4 us
    all_to_all x1, starting transfers between devices, body(): received = lax.all_to_all(payload, 'src', 0, 0, tiled=True)  18.1 us
    gather x2, local copies, waits for them, and re-layouts, body(): negs_in = every_dst[span_in].reshape(n_src, nch * part, width)  14.4 us
    all_to_all x1, starting transfers between devices, body(): back_rows = lax.all_to_all(back_rows, 'src', 0, 0, tiled=True)  12.9 us
  transfers between devices with their start and end apart: 17, of which 13 were waited for; matrix products, arithmetic and copies ran while one was open for 25% of the time, Pallas kernels for 0%

profile of v2, /device:TPU:4, one launch (start us, length us, event | category | flops | bytes accessed | tf_op | source)
XLA Modules:
  0.0 528.1 jit_solution(5397476905979356002)
XLA Ops:
  12.0 4.0 gather_fusion
  17.2 18.1 %all-to-all-start = ((bf16[16,65,400]{2,1,0:T(8,128)(2,1)}), bf16[16,65,400]{2,1,0:T(8,128)(2,1)S(1)}, u32[]{:S(2)}, u32[]{:S(2)}) async-start(bf16[16,65,400]{2,1,0:T(8,128)(2,1)} %pad_maximum_fusion.3), calls=%async_computation | async-start | bytes 2359296 | tf_op jit(solution)/shard_map/all_to_all | solution.py:100
  35.4 59.2 %all-to-all-done = bf16[16,65,400]{2,1,0:T(8,128)(2,1)S(1)} async-done(((bf16[16,65,400]{2,1,0:T(8,128)(2,1)}), bf16[16,65,400]{2,1,0:T(8,128)(2,1)S(1)}, u32[]{:S(2)}, u32[]{:S(2)}) %all-to-all-start) | async-done | bytes 832032 | tf_op jit(solution)/shard_map/all_to_all | solution.py:100
  94.8 5.1 gather_fusion.1
  104.2 9.4 %all-to-all-start.2 = ((bf16[16,4,16,400]{3,2,1,0:T(8,128)(2,1)}), bf16[16,4,16,400]{3,2,1,0:T(8,128)(2,1)S(1)}, u32[]{:S(2)}, u32[]{:S(2)}) async-start(bf16[16,4,16,400]{3,2,1,0:T(8,128)(2,1)} %copy.81), calls=%async_computation.2 | async-start | bytes 2097152 | tf_op jit(solution)/shard_map/all_to_all | solution.py:110
  113.7 5.1 gather_fusion.4
  119.2 71.0 %all-gather.3.cloned.1.call-done = bf16[8192,400]{0,1:T(8,128)(2,1)} async-done(((bf16[256,400]{0,1:T(8,128)(2,1)}), bf16[8192,400]{0,1:T(8,128)(2,1)}) %all-gather.3.cloned.1.call-update) | async-done | bytes 6553616 | tf_op jit(solution)/shard_map/all_gather | solution.py:87
  190.2 6.0 %copy.121 = bf16[50,32,8,256]{3,2,0,1:T(8,128)(2,1)} copy(bf16[50,32,8,256]{3,2,1,0:T(8,128)(2,1)} %bitcast.196) | data formatting | bytes 13107200 | tf_op jit(solution)/shard_map/all_gather | solution.py:87
  196.3 6.5 %gather_fusion.2 = bf16[32,256,400]{1,2,0:T(8,128)(2,1)} fusion(bf16[32,256,400]{1,2,0:T(8,128)(2,1)} %bitcast.188, s32[1024]{0:T(1024)S(1)} %pad_clamp_fusion.6), kind=kCustom, calls=%fused_computation.2 | custom fusion | bytes 13107328 | tf_op jit(solution)/shard_map/gather | solution.py:114
  202.8 7.9 %copy.83 = bf16[32,256,400]{1,0,2:T(8,128)(2,1)} copy(bf16[32,256,400]{1,2,0:T(8,128)(2,1)} %gather_fusion.2) | data formatting | bytes 13107200 | tf_op jit(solution)/shard_map/gather | solution.py:114
  210.7 11.1 %reshape.702 = bf16[16,512,400]{1,0,2:T(8,128)(2,1)} reshape(bf16[32,256,400]{1,0,2:T(8,128)(2,1)} %copy.83) | data formatting | bytes 13107200 | tf_op jit(solution)/shard_map/reshape | solution.py:114
  221.8 10.4 %fusion.68 = (f32[16,64]{1,0:T(8,128)S(1)}, f32[16,64,512]{2,1,0:T(8,128)S(1)}) fusion(bf16[16,64,400]{2,1,0:T(8,128)(2,1)} %bitcast.195, bf16[16,512,400]{1,0,2:T(8,128)(2,1)} %reshape.702), kind=kOutput, calls=%fused_computation.224 | convolution fusion | flops 419953664 | bytes 9474048 | tf_op jit(solution)/shard_map/...md,...nd->...mn/dot_general | solution.py:60
  233.9 8.5 %add_convert_fusion = bf16[16,64,400]{2,1,0:T(8,128)(2,1)S(1)} fusion(f32[16,64,400]{2,1,0:T(8,128)S(1)} %bitcast.191, bf16[16,512,400]{1,0,2:T(8,128)(2,1)S(1)} %bitcast.187, f32[16,64,512]{2,1,0:T(8,128)S(1)} %get-tuple-element.159, f32[16,64]{1,0:T(8,128)S(1)} %convert_divide_fusion, f32[16,64]{1,0:T(8,128)S(1)} %get-tuple-element.88, f32[16,64]{1,0:T(8,128)S(1)} %max.26), kind=kOutput, calls=%fused_computation.31 | convolution fusion | flops 422232064 | bytes 11120640 | tf_op jit(solution)/shard_map/pmn,pnd->pmd/dot_general | solution.py:120
  244.6 12.9 %all-to-all-start.1 = ((bf16[16,4,16,400]{3,2,1,0:T(8,128)(2,1)}), bf16[16,4,16,400]{3,2,1,0:T(8,128)(2,1)}, u32[]{:S(2)}, u32[]{:S(2)}) async-start(bf16[16,4,16,400]{3,2,1,0:T(8,128)(2,1)} %copy.87), calls=%async_computation.1 | async-start | bytes 2097152 | tf_op jit(solution)/shard_map/all_to_all | solution.py:129
  260.5 4.3 compare_select_fusion.5
  270.6 35.3 %add_select_fusion.2 = (f32[1024]{0:T(1024)S(1)}, pred[1024]{0:T(1024)(128)(4,1)S(1)}) fusion(f32[1024]{0:T(1024)S(1)} %fusion.12, f32[1024]{0:T(1024)S(1)} %reduce_sum.44, f32[1024]{0:T(1024)S(1)} %max.27, pred[1024]{0:T(1024)(128)(4,1)S(1)} %get-tuple-element.83, pred[1024]{0:T(1024)(128)(4,1)S(1)} %get-tuple-element.82, ...), kind=kLoop, calls=%fused_computation.172 | loop fusion | flops 79872 | bytes 84228 | tf_op jit(solution)/shard_map/mul | solution.py:67
  306.7 7.3 %scatter_custom_fusion = f32[256,400]{1,0:T(8,128)S(1)} fusion(s32[1024]{0:T(1024)} %bitcast.228, bf16[1024,400]{1,0:T(8,128)(2,1)} %bitcast.124, f32[]{:T(128)} %constant.229.clone.1), kind=kCustom, calls=%fused_computation.22 | custom fusion | flops 819200 | bytes 1458688 | tf_op jit(solution)/shard_map/scatter-add | solution.py:131
  326.7 4.0 collective-permute-start.2
  337.2 6.4 %collective-permute-done.3 = bf16[768,400]{0,1:T(8,128)(2,1)S(1)} collective-permute-done((bf16[768,400]{0,1:T(8,128)(2,1)}, bf16[768,400]{0,1:T(8,128)(2,1)S(1)}, u32[]{:S(2)}, u32[]{:S(2)}) %collective-permute-start.3) | collective-permute-done | bytes 614432 | tf_op jit(solution)/shard_map/ppermute | solution.py:34
  347.4 12.3 %collective-permute-done.1 = bf16[768,400]{0,1:T(8,128)(2,1)} collective-permute-done((bf16[768,400]{0,1:T(8,128)(2,1)}, bf16[768,400]{0,1:T(8,128)(2,1)}, u32[]{:S(2)}, u32[]{:S(2)}) %collective-permute-start.1) | collective-permute-done | bytes 614432 | tf_op jit(solution)/shard_map/ppermute | solution.py:34
  362.7 3.8 gather_fusion.6
  371.0 7.2 %collective-permute-start.5 = (bf16[768,400]{0,1:T(8,128)(2,1)S(1)}, bf16[768,400]{0,1:T(8,128)(2,1)S(1)}, u32[]{:S(2)}, u32[]{:S(2)}) collective-permute-start(bf16[768,400]{0,1:T(8,128)(2,1)S(1)} %fusion.77), channel_id=1, source_target_pairs={{0,16},{1,17},{2,18},{3,19},{4,20},{5,21},{6,22},{7,23},{8,24},{9,... | collective-permute-start | bytes 1843208 | tf_op jit(solution)/shard_map/ppermute | solution.py:34
  382.2 6.6 %collective-permute-done.6 = bf16[768,400]{0,1:T(8,128)(2,1)S(1)} collective-permute-done((bf16[768,400]{0,1:T(8,128)(2,1)S(1)}, bf16[768,400]{0,1:T(8,128)(2,1)S(1)}, u32[]{:S(2)}, u32[]{:S(2)}) %collective-permute-start.6) | collective-permute-done | bytes 614432 | tf_op jit(solution)/shard_map/ppermute | solution.py:34
  388.8 40.7 %collective-permute-done.5 = bf16[768,400]{0,1:T(8,128)(2,1)S(1)} collective-permute-done((bf16[768,400]{0,1:T(8,128)(2,1)S(1)}, bf16[768,400]{0,1:T(8,128)(2,1)S(1)}, u32[]{:S(2)}, u32[]{:S(2)}) %collective-permute-start.5) | collective-permute-done | bytes 614432 | tf_op jit(solution)/shard_map/ppermute | solution.py:34
  438.8 7.4 %scatter_custom_fusion.1 = f32[256,400]{1,0:T(8,128)S(1)} fusion(f32[256,400]{1,0:T(8,128)S(1)} %copy.95, s32[1024]{0:T(1024)S(1)} %bitcast.224, bf16[1024,400]{1,0:T(8,128)(2,1)S(1)} %bitcast.194, f32[1024]{0:T(1024)S(1)} %get-tuple-element.84), kind=kCustom, calls=%fused_computation.26 | custom fusion | flops 1228800 | bytes 1462272 | tf_op jit(solution)/shard_map/scatter-add | solution.py:143
  448.3 4.4 collective-permute-start.7
  463.9 7.3 %collective-permute-start.12 = (bf16[256,400]{1,0:T(8,128)(2,1)S(1)}, bf16[256,400]{1,0:T(8,128)(2,1)S(1)}, u32[]{:S(2)}, u32[]{:S(2)}) collective-permute-start(bf16[256,400]{1,0:T(8,128)(2,1)S(1)} %fusion.76), channel_id=1, source_target_pairs={{0,384},{32,416},{64,448},{96,480},{128,0},{160,32},{192,64},{224,... | collective-permute-start | bytes 614408 | tf_op jit(solution)/shard_map/ppermute | solution.py:34
  471.2 7.3 %collective-permute-start.11 = (bf16[256,400]{1,0:T(8,128)(2,1)S(1)}, bf16[256,400]{1,0:T(8,128)(2,1)S(1)}, u32[]{:S(2)}, u32[]{:S(2)}) collective-permute-start(bf16[256,400]{1,0:T(8,128)(2,1)S(1)} %fusion.76), channel_id=1, source_target_pairs={{0,256},{32,288},{64,320},{96,352},{128,384},{160,416},{192,448},{... | collective-permute-start | bytes 614408 | tf_op jit(solution)/shard_map/ppermute | solution.py:34
  478.5 7.3 %collective-permute-start.10 = (bf16[256,400]{1,0:T(8,128)(2,1)S(1)}, bf16[256,400]{1,0:T(8,128)(2,1)S(1)}, u32[]{:S(2)}, u32[]{:S(2)}) collective-permute-start(bf16[256,400]{1,0:T(8,128)(2,1)S(1)} %fusion.76), channel_id=1, source_target_pairs={{0,128},{32,160},{64,192},{96,224},{128,256},{160,288},{192,320},{... | collective-permute-start | bytes 614408 | tf_op jit(solution)/shard_map/ppermute | solution.py:34
  485.9 20.1 %collective-permute-done.12 = bf16[256,400]{1,0:T(8,128)(2,1)S(1)} collective-permute-done((bf16[256,400]{1,0:T(8,128)(2,1)S(1)}, bf16[256,400]{1,0:T(8,128)(2,1)S(1)}, u32[]{:S(2)}, u32[]{:S(2)}) %collective-permute-start.12) | collective-permute-done | bytes 204832 | tf_op jit(solution)/shard_map/ppermute | solution.py:34
  506.1 5.2 collective-permute-done.11
  511.2 7.5 %collective-permute-done.10 = bf16[256,400]{1,0:T(8,128)(2,1)S(1)} collective-permute-done((bf16[256,400]{1,0:T(8,128)(2,1)S(1)}, bf16[256,400]{1,0:T(8,128)(2,1)S(1)}, u32[]{:S(2)}, u32[]{:S(2)}) %collective-permute-start.10) | collective-permute-done | bytes 204832 | tf_op jit(solution)/shard_map/ppermute | solution.py:34
  (156 shorter events, 82.0 us)
Async XLA Ops:
  7.2 94.4 %copy-start = (bf16[4,400,400]{2,1,0:T(8,128)(2,1)S(1)}, bf16[4,400,400]{2,1,0:T(8,128)(2,1)}, u32[]{:S(2)}) copy-start(bf16[4,400,400]{2,1,0:T(8,128)(2,1)} %param.9) | copy-start | bytes 3840004
  7.2 183.1 %all-gather.3.cloned.1.call-start = ((), (), s32[]{:S(2)}) async-start(), calls=%async_computation.3 | async-start | bytes 6758400 | tf_op jit(solution)/shard_map/all_gather | solution.py:87
  16.0 19.3 %copy-start.12 = (bf16[256,400]{0,1:T(8,128)(2,1)S(1)}, bf16[256,400]{0,1:T(8,128)(2,1)}, u32[]{:S(2)}) copy-start(bf16[256,400]{0,1:T(8,128)(2,1)} %param.11) | copy-start | bytes 614404
  17.2 77.4 %all-to-all-start = ((bf16[16,65,400]{2,1,0:T(8,128)(2,1)}), bf16[16,65,400]{2,1,0:T(8,128)(2,1)S(1)}, u32[]{:S(2)}, u32[]{:S(2)}) async-start(bf16[16,65,400]{2,1,0:T(8,128)(2,1)} %pad_maximum_fusion.3), calls=%async_computation | async-start | bytes 2359296 | tf_op jit(solution)/shard_map/all_to_all | solution.py:100
  101.5 1.6 copy-start.6
  103.1 10.6 %copy-start.14 = (s32[1,1,1024]{2,1,0:T(1,128)S(1)}, s32[1,1,1024]{2,1,0:T(1,128)}, u32[]{:S(2)}) copy-start(s32[1,1,1024]{2,1,0:T(1,128)} %param.13) | copy-start | bytes 12292
  104.2 140.4 %all-to-all-start.2 = ((bf16[16,4,16,400]{3,2,1,0:T(8,128)(2,1)}), bf16[16,4,16,400]{3,2,1,0:T(8,128)(2,1)S(1)}, u32[]{:S(2)}, u32[]{:S(2)}) async-start(bf16[16,4,16,400]{3,2,1,0:T(8,128)(2,1)} %copy.81), calls=%async_computation.2 | async-start | bytes 2097152 | tf_op jit(solution)/shard_map/all_to_all | solution.py:110
  221.8 11.3 %slice-start = ((s8[6553600]{0:T(1024)(128)(4,1)}), s8[4194304]{0:T(1024)(128)(4,1)S(1)}, s32[]{:S(2)}) async-start(s8[6553600]{0:T(1024)(128)(4,1)} %bitcast.186), calls=%async_computation.4 | async-start | bytes 8388608
  221.8 11.3 %slice-start.1 = ((s8[6553600]{0:T(1024)(128)(4,1)}), s8[2359296]{0:T(1024)(128)(4,1)S(1)}, s32[]{:S(2)}) async-start(s8[6553600]{0:T(1024)(128)(4,1)} %bitcast.186), calls=%async_computation.5 | async-start | bytes 4718592
  232.3 1.6 copy-start.4
  243.4 14.1 %copy-start.15 = (s32[1,2]{1,0:T(1,128)S(1)}, s32[1,2]{1,0:T(1,128)}, u32[]{:S(2)}) copy-start(s32[1,2]{1,0:T(1,128)} %param.15) | copy-start | bytes 28
  243.4 14.1 %copy-start.9 = (s32[1,1,64]{2,1,0:T(1,128)S(1)}, s32[1,1,64]{2,1,0:T(1,128)}, u32[]{:S(2)}) copy-start(s32[1,1,64]{2,1,0:T(1,128)} %param.14) | copy-start | bytes 772
  243.4 17.0 %copy-start.13 = (s32[8,128]{1,0:T(8,128)S(1)}, s32[8,128]{1,0:T(8,128)}, u32[]{:S(2)}) copy-start(s32[8,128]{1,0:T(8,128)} %constant.236.clone.1) | copy-start | bytes 12292
  243.4 22.2 %copy-start.5 = (bf16[1024,400]{1,0:T(8,128)(2,1)S(1)}, bf16[1024,400]{1,0:T(8,128)(2,1)}, u32[]{:S(2)}) copy-start(bf16[1024,400]{1,0:T(8,128)(2,1)} %gather_fusion.4) | copy-start | bytes 2457604
  244.6 62.2 %all-to-all-start.1 = ((bf16[16,4,16,400]{3,2,1,0:T(8,128)(2,1)}), bf16[16,4,16,400]{3,2,1,0:T(8,128)(2,1)}, u32[]{:S(2)}, u32[]{:S(2)}) async-start(bf16[16,4,16,400]{3,2,1,0:T(8,128)(2,1)} %copy.87), calls=%async_computation.1 | async-start | bytes 2097152 | tf_op jit(solution)/shard_map/all_to_all | solution.py:129
  315.1 4.1 collective-permute-start
  322.4 1.4 copy-start.2
  324.8 18.8 %collective-permute-start.3 = (bf16[768,400]{0,1:T(8,128)(2,1)}, bf16[768,400]{0,1:T(8,128)(2,1)S(1)}, u32[]{:S(2)}, u32[]{:S(2)}) collective-permute-start(bf16[768,400]{0,1:T(8,128)(2,1)} %fusion.78), channel_id=1, source_target_pairs={{0,6},{1,7},{2,0},{3,1},{4,2},{5,3},{6,4},{7,5},{8,14},{9,15},{10,... | collective-permute-start | bytes 1843208 | tf_op jit(solution)/shard_map/ppermute | solution.py:34
  326.7 20.7 %collective-permute-start.2 = (bf16[768,400]{0,1:T(8,128)(2,1)}, bf16[768,400]{0,1:T(8,128)(2,1)}, u32[]{:S(2)}, u32[]{:S(2)}) collective-permute-start(bf16[768,400]{0,1:T(8,128)(2,1)} %fusion.78), channel_id=1, source_target_pairs={{0,4},{1,5},{2,6},{3,7},{4,0},{5,1},{6,2},{7,3},{8,12},{9,13},{10,... | collective-permute-start | bytes 1843208 | tf_op jit(solution)/shard_map/ppermute | solution.py:34
  330.7 29.0 %collective-permute-start.1 = (bf16[768,400]{0,1:T(8,128)(2,1)}, bf16[768,400]{0,1:T(8,128)(2,1)}, u32[]{:S(2)}, u32[]{:S(2)}) collective-permute-start(bf16[768,400]{0,1:T(8,128)(2,1)} %fusion.78), channel_id=1, source_target_pairs={{0,2},{1,3},{2,4},{3,5},{4,6},{5,7},{6,0},{7,1},{8,10},{9,11},{10,... | collective-permute-start | bytes 1843208 | tf_op jit(solution)/shard_map/ppermute | solution.py:34
  368.7 11.5 %copy-start.7 = (bf16[16,64,400]{2,1,0:T(8,128)(2,1)S(1)}, bf16[16,64,400]{2,1,0:T(8,128)(2,1)}, u32[]{:S(2)}) copy-start(bf16[16,64,400]{2,1,0:T(8,128)(2,1)} %copy-done.6) | copy-start | bytes 2457604
  368.7 11.5 %copy-start.11 = (bf16[16,64,400]{2,1,0:T(8,128)(2,1)S(1)}, bf16[16,64,400]{2,1,0:T(8,128)(2,1)}, u32[]{:S(2)}) copy-start(bf16[16,64,400]{2,1,0:T(8,128)(2,1)} %copy-done.10) | copy-start | bytes 2457604
  368.9 19.9 %collective-permute-start.6 = (bf16[768,400]{0,1:T(8,128)(2,1)S(1)}, bf16[768,400]{0,1:T(8,128)(2,1)S(1)}, u32[]{:S(2)}, u32[]{:S(2)}) collective-permute-start(bf16[768,400]{0,1:T(8,128)(2,1)S(1)} %fusion.77), channel_id=1, source_target_pairs={{0,24},{1,25},{2,26},{3,27},{4,28},{5,29},{6,30},{7,31},{8,0},{9,1... | collective-permute-start | bytes 1843208 | tf_op jit(solution)/shard_map/ppermute | solution.py:34
  371.0 58.5 %collective-permute-start.5 = (bf16[768,400]{0,1:T(8,128)(2,1)S(1)}, bf16[768,400]{0,1:T(8,128)(2,1)S(1)}, u32[]{:S(2)}, u32[]{:S(2)}) collective-permute-start(bf16[768,400]{0,1:T(8,128)(2,1)S(1)} %fusion.77), channel_id=1, source_target_pairs={{0,16},{1,17},{2,18},{3,19},{4,20},{5,21},{6,22},{7,23},{8,24},{9,... | collective-permute-start | bytes 1843208 | tf_op jit(solution)/shard_map/ppermute | solution.py:34
  378.2 51.3 %collective-permute-start.4 = (bf16[768,400]{0,1:T(8,128)(2,1)S(1)}, bf16[768,400]{0,1:T(8,128)(2,1)S(1)}, u32[]{:S(2)}, u32[]{:S(2)}) collective-permute-start(bf16[768,400]{0,1:T(8,128)(2,1)S(1)} %fusion.77), channel_id=1, source_target_pairs={{0,8},{1,9},{2,10},{3,11},{4,12},{5,13},{6,14},{7,15},{8,16},{9,17... | collective-permute-start | bytes 1843208 | tf_op jit(solution)/shard_map/ppermute | solution.py:34
  446.2 12.6 %collective-permute-start.8 = (bf16[256,400]{1,0:T(8,128)(2,1)S(1)}, bf16[256,400]{1,0:T(8,128)(2,1)S(1)}, u32[]{:S(2)}, u32[]{:S(2)}) collective-permute-start(bf16[256,400]{1,0:T(8,128)(2,1)S(1)} %convert_element_type.182), channel_id=1, source_target_pairs={{0,64},{32,96},{64,0},{96,32},{128,192},{160,224},{192,128},{224,1... | collective-permute-start | bytes 614408 | tf_op jit(solution)/shard_map/ppermute | solution.py:34
  448.3 14.3 %collective-permute-start.7 = (bf16[256,400]{1,0:T(8,128)(2,1)S(1)}, bf16[256,400]{1,0:T(8,128)(2,1)S(1)}, u32[]{:S(2)}, u32[]{:S(2)}) collective-permute-start(bf16[256,400]{1,0:T(8,128)(2,1)S(1)} %convert_element_type.182), channel_id=1, source_target_pairs={{0,32},{32,64},{64,96},{96,0},{128,160},{160,192},{192,224},{224,1... | collective-permute-start | bytes 614408 | tf_op jit(solution)/shard_map/ppermute | solution.py:34
  452.7 9.9 %collective-permute-start.9 = (bf16[256,400]{1,0:T(8,128)(2,1)S(1)}, bf16[256,400]{1,0:T(8,128)(2,1)S(1)}, u32[]{:S(2)}, u32[]{:S(2)}) collective-permute-start(bf16[256,400]{1,0:T(8,128)(2,1)S(1)} %convert_element_type.182), channel_id=1, source_target_pairs={{0,96},{32,0},{64,32},{96,64},{128,224},{160,128},{192,160},{224,1... | collective-permute-start | bytes 614408 | tf_op jit(solution)/shard_map/ppermute | solution.py:34
  463.9 42.2 %collective-permute-start.12 = (bf16[256,400]{1,0:T(8,128)(2,1)S(1)}, bf16[256,400]{1,0:T(8,128)(2,1)S(1)}, u32[]{:S(2)}, u32[]{:S(2)}) collective-permute-start(bf16[256,400]{1,0:T(8,128)(2,1)S(1)} %fusion.76), channel_id=1, source_target_pairs={{0,384},{32,416},{64,448},{96,480},{128,0},{160,32},{192,64},{224,... | collective-permute-start | bytes 614408 | tf_op jit(solution)/shard_map/ppermute | solution.py:34
  471.2 40.1 %collective-permute-start.11 = (bf16[256,400]{1,0:T(8,128)(2,1)S(1)}, bf16[256,400]{1,0:T(8,128)(2,1)S(1)}, u32[]{:S(2)}, u32[]{:S(2)}) collective-permute-start(bf16[256,400]{1,0:T(8,128)(2,1)S(1)} %fusion.76), channel_id=1, source_target_pairs={{0,256},{32,288},{64,320},{96,352},{128,384},{160,416},{192,448},{... | collective-permute-start | bytes 614408 | tf_op jit(solution)/shard_map/ppermute | solution.py:34
  478.5 40.3 %collective-permute-start.10 = (bf16[256,400]{1,0:T(8,128)(2,1)S(1)}, bf16[256,400]{1,0:T(8,128)(2,1)S(1)}, u32[]{:S(2)}, u32[]{:S(2)}) collective-permute-start(bf16[256,400]{1,0:T(8,128)(2,1)S(1)} %fusion.76), channel_id=1, source_target_pairs={{0,128},{32,160},{64,192},{96,224},{128,256},{160,288},{192,320},{... | collective-permute-start | bytes 614408 | tf_op jit(solution)/shard_map/ppermute | solution.py:34
  519.5 1.4 copy-start.1
  (3 other events, 3.4 us)
Sparse Core Ops, SparseCore 0:
  10.0 180.1 all-gather.2

commit v3 on v2

v3 whole, which is shorter than its diff:
```python
import jax
import jax.numpy as jnp
from jax import lax
from jax.sharding import PartitionSpec as P

F32 = jnp.float32
BF16 = jnp.bfloat16


def butterfly_sum(x, axis, bits):
    n = lax.axis_size(axis)
    for bit in bits:
        low = x.astype(BF16)
        other = lax.ppermute(low, axis, [(i, i ^ bit) for i in range(n)])
        x = low.astype(F32) + other.astype(F32)
    return x


def axis_bits(n):
    return [1 << b for b in range(n.bit_length() - 1)]


def group_round(x, axis, stride, size):
    n = lax.axis_size(axis)
    me = lax.axis_index(axis)
    member = (me // stride) % size
    low = x.astype(BF16)
    got = [low]
    for shift in range(1, size):
        perm = []
        for i in range(n):
            m = (i // stride) % size
            perm.append((i, i + (((m + shift) % size) - m) * stride))
        got.append(lax.ppermute(low, axis, perm))
    stacked = jnp.stack(got)
    order = (member - jnp.arange(size)) % size
    ordered = stacked[order].astype(F32)
    total = ordered[0]
    for j in range(1, size):
        total = total + ordered[j]
    return total


def sub_axes(n):
    shapes = {32: ((1, 2), (2, 4), (8, 4)), 16: ((1, 4), (4, 4))}
    return shapes.get(n)


def axis_sum(x, axis):
    n = lax.axis_size(axis)
    parts = sub_axes(n)
    if parts is None:
        return butterfly_sum(x, axis, axis_bits(n))
    for stride, size in parts:
        x = group_round(x, axis, stride, size)
    return x


def softmax_grads(z, y, negs, live):
    neg = jnp.einsum("...md,...nd->...mn", z, negs, preferred_element_type=F32)
    pos = jnp.sum(z.astype(F32) * y.astype(F32), -1)
    row_max = jnp.maximum(jnp.max(neg, -1), pos)
    exp_neg = jnp.exp(neg - row_max[..., None])
    exp_pos = jnp.exp(pos - row_max)
    denom = jnp.sum(exp_neg, -1) + exp_pos
    g_neg = (exp_neg * (live / denom)[..., None]).astype(BF16)
    g_pos = (exp_pos / denom - 1.0) * live
    return g_neg, g_pos


def body(rel_ops, src_emb, dst_emb, edge_src, edge_dst, slot_count, neg_span):
    n_src = lax.axis_size("src")
    n_dst = lax.axis_size("dst")
    rk = rel_ops.shape[0]
    width = rel_ops.shape[1]
    part = src_emb.shape[0]
    slots = edge_src.shape[2]
    cap = slots // (n_src * rk)
    nch = neg_span.shape[1]
    ids_src = edge_src.reshape(slots)
    ids_dst = edge_dst.reshape(slots)
    counts = slot_count.reshape(n_src * rk)
    spans = neg_span.reshape(nch)
    own_dst = lax.axis_index("dst")
    dst_bits = axis_bits(n_dst)

    pieces = jnp.stack(
        [jnp.where(spans[i] == own_dst, dst_emb, jnp.zeros_like(dst_emb)) for i in range(nch)]
    )
    negs = butterfly_sum(pieces, "dst", dst_bits).astype(BF16).reshape(nch * part, width)

    inputs = src_emb[ids_src].reshape(n_src, rk, cap, width)
    x_in = lax.all_to_all(inputs, "src", 0, 0, tiled=True)
    mapped = jnp.einsum(
        "pkcd,kde->pkce", x_in, rel_ops, preferred_element_type=F32
    ).astype(BF16)
    z_b = lax.all_to_all(mapped, "src", 0, 0, tiled=True).reshape(slots, width)

    y_b = dst_emb[ids_dst]
    lane = jnp.arange(cap, dtype=jnp.int32)
    live = (lane[None, :] < counts[:, None]).astype(F32).reshape(slots)
    g_neg, g_pos = softmax_grads(z_b, y_b, negs, live)
    upstream = (
        g_pos[:, None] * y_b.astype(F32)
        + jnp.dot(g_neg, negs, preferred_element_type=F32)
    ).astype(BF16)
    u_in = lax.all_to_all(
        upstream.reshape(n_src, rk, cap, width), "src", 0, 0, tiled=True
    )
    grad_rel = jnp.einsum(
        "pkcd,pkce->kde", x_in, u_in, preferred_element_type=F32
    ).astype(BF16)
    back_rows = jnp.einsum(
        "pkce,kde->pkcd", u_in, rel_ops, preferred_element_type=F32
    ).astype(BF16)
    back_rows = lax.all_to_all(back_rows, "src", 0, 0, tiled=True)

    dst_local = jax.ops.segment_sum(
        g_pos[:, None] * z_b.astype(F32), ids_dst, num_segments=part
    )
    span_grad = jnp.einsum("bn,bd->nd", g_neg, z_b, preferred_element_type=F32)
    span_sum = butterfly_sum(span_grad, "dst", dst_bits)
    for index in range(nch):
        piece = span_sum[index * part : (index + 1) * part]
        dst_local = dst_local + jnp.where(spans[index] == own_dst, piece, 0.0)
    grad_dst = butterfly_sum(dst_local, "src", axis_bits(n_src)).astype(BF16)

    src_local = jax.ops.segment_sum(
        back_rows.reshape(slots, width).astype(F32), ids_src, num_segments=part
    )
    grad_src = butterfly_sum(src_local, "dst", dst_bits).astype(BF16)
    return (grad_rel, grad_src, grad_dst)


def solution(mesh):
    placed = (
        P(("src", "dst"), None, None),
        P("src", None),
        P("dst", None),
        P("src", "dst", None),
        P("src", "dst", None),
        P("src", "dst", None),
        P("src", None),
    )
    return jax.shard_map(
        body,
        mesh=mesh,
        in_specs=placed,
        out_specs=(P(("src", "dst"), None, None), P("src", None), P("dst", None)),
        check_vma=False,
    )
```

time: 536 us -> 445 us (0.83)
  the two profiles are of different devices: /device:TPU:4 before, /device:TPU:1 now
where the time goes in v3:
time: 445 us; the launch traced here: 443 us
  waiting for transfers between devices  247 us (56%)
  starting transfers between devices  129 us (29%)
  local copies, waits for them, and re-layouts  27.2 us (6%)
  other arithmetic  26.9 us (6%)
  matrix products  11.4 us (3%)
    ppermute x19, waiting for transfers between devices, butterfly_sum(): other = lax.ppermute(low, axis, [(i, i ^ bit) for i in range(n)])  166 us
    ppermute x19, starting transfers between devices, butterfly_sum(): other = lax.ppermute(low, axis, [(i, i ^ bit) for i in range(n)])  70.9 us
    all_to_all x1, waiting for transfers between devices, body(): lax.all_to_all(upstream.reshape(n_src, rk, cap, width), 'src', 0, 0, tile...  41.1 us
    all_to_all x1, waiting for transfers between devices, body(): x_in = lax.all_to_all(inputs, 'src', 0, 0, tiled=True)  39.4 us
    all_to_all x1, starting transfers between devices, body(): x_in = lax.all_to_all(inputs, 'src', 0, 0, tiled=True)  18.3 us
    all_to_all x1, starting transfers between devices, body(): z_b = lax.all_to_all(mapped, 'src', 0, 0, tiled=True).reshape(slots, width)  15.6 us
    all_to_all x1, starting transfers between devices, body(): lax.all_to_all(upstream.reshape(n_src, rk, cap, width), 'src', 0, 0, tile...  15.1 us
  transfers between devices with their start and end apart: 23, of which 14 were waited for; matrix products, arithmetic and copies ran while one was open for 11% of the time, Pallas kernels for 0%

profile of v3, /device:TPU:1, one launch (start us, length us, event | category | flops | bytes accessed | tf_op | source)
XLA Modules:
  0.0 443.2 jit_solution(11817631926669344186)
XLA Ops:
  2.5 5.1 %gather_fusion = bf16[1024,400]{1,0:T(8,128)(2,1)} fusion(bf16[256,400]{1,0:T(8,128)(2,1)S(1)} %copy.54, s32[1024]{0:T(1024)S(1)} %broadcast_clamp_fusion.1), kind=kCustom, calls=%fused_computation | custom fusion | bytes 1642496 | tf_op jit(solution)/shard_map/gather | solution.py:92
  7.6 18.3 %all-to-all-start = ((bf16[16,4,16,400]{3,2,1,0:T(8,128)(2,1)}), bf16[16,4,16,400]{3,2,1,0:T(8,128)(2,1)S(1)}, u32[]{:S(2)}, u32[]{:S(2)}) async-start(bf16[16,4,16,400]{3,2,1,0:T(8,128)(2,1)} %bitcast.2), calls=%async_computation | async-start | bytes 2097152 | tf_op jit(solution)/shard_map/all_to_all | solution.py:93
  31.6 39.4 %all-to-all-done = bf16[16,4,16,400]{3,2,1,0:T(8,128)(2,1)S(1)} async-done(((bf16[16,4,16,400]{3,2,1,0:T(8,128)(2,1)}), bf16[16,4,16,400]{3,2,1,0:T(8,128)(2,1)S(1)}, u32[]{:S(2)}, u32[]{:S(2)}) %all-to-all-start) | async-done | bytes 819232 | tf_op jit(solution)/shard_map/all_to_all | solution.py:93
  72.7 15.6 %all-to-all-start.1 = ((bf16[16,4,16,400]{3,2,1,0:T(8,128)(2,1)}), bf16[16,4,16,400]{3,2,1,0:T(8,128)(2,1)S(1)}, u32[]{:S(2)}, u32[]{:S(2)}) async-start(bf16[16,4,16,400]{3,2,1,0:T(8,128)(2,1)} %copy.56), calls=%async_computation.1 | async-start | bytes 2097152 | tf_op jit(solution)/shard_map/all_to_all | solution.py:97
  88.5 3.2 collective-permute-start.1
  91.7 8.5 %collective-permute-done.1 = bf16[2,256,400]{1,2,0:T(8,128)(2,1)S(1)} collective-permute-done((bf16[2,256,400]{1,2,0:T(8,128)(2,1)S(1)}, bf16[2,256,400]{1,2,0:T(8,128)(2,1)S(1)}, u32[]{:S(2)}, u32[]{:S(2)}) %collective-permute-start.1) | collective-permute-done | bytes 409632 | tf_op jit(solution)/shard_map/ppermute | solution.py:14
  100.4 4.8 %collective-permute-start.2 = (bf16[2,256,400]{1,2,0:T(8,128)(2,1)S(1)}, bf16[2,256,400]{1,2,0:T(8,128)(2,1)S(1)}, u32[]{:S(2)}, u32[]{:S(2)}) collective-permute-start(bf16[2,256,400]{1,2,0:T(8,128)(2,1)S(1)} %add_convert_fusion.8), channel_id=1, source_target_pairs={{0,4},{1,5},{2,6},{3,7},{4,0},{5,1},{6,2},{7,3},{8,12},{9,13},{10,... | collective-permute-start | bytes 1228808 | tf_op jit(solution)/shard_map/ppermute | solution.py:14
  105.2 7.5 %collective-permute-done.2 = bf16[2,256,400]{1,2,0:T(8,128)(2,1)S(1)} collective-permute-done((bf16[2,256,400]{1,2,0:T(8,128)(2,1)S(1)}, bf16[2,256,400]{1,2,0:T(8,128)(2,1)S(1)}, u32[]{:S(2)}, u32[]{:S(2)}) %collective-permute-start.2) | collective-permute-done | bytes 409632 | tf_op jit(solution)/shard_map/ppermute | solution.py:14
  116.4 26.0 %collective-permute-done.3 = bf16[2,256,400]{1,2,0:T(8,128)(2,1)} collective-permute-done((bf16[2,256,400]{1,2,0:T(8,128)(2,1)S(1)}, bf16[2,256,400]{1,2,0:T(8,128)(2,1)}, u32[]{:S(2)}, u32[]{:S(2)}) %collective-permute-start.3) | collective-permute-done | bytes 409632 | tf_op jit(solution)/shard_map/ppermute | solution.py:14
  144.3 3.3 collective-permute-start.4
  147.6 5.0 %gather_fusion.1 = bf16[1024,400]{1,0:T(8,128)(2,1)} fusion(bf16[256,400]{1,0:T(8,128)(2,1)S(1)} %copy.57, s32[1024]{0:T(1024)S(1)} %broadcast_clamp_fusion), kind=kCustom, calls=%fused_computation.1 | custom fusion | bytes 1642496 | tf_op jit(solution)/shard_map/gather | solution.py:99
  155.7 10.4 %collective-permute-done.4 = bf16[2,256,400]{1,2,0:T(8,128)(2,1)} collective-permute-done((bf16[2,256,400]{1,2,0:T(8,128)(2,1)}, bf16[2,256,400]{1,2,0:T(8,128)(2,1)}, u32[]{:S(2)}, u32[]{:S(2)}) %collective-permute-start.4) | collective-permute-done | bytes 409632 | tf_op jit(solution)/shard_map/ppermute | solution.py:14
  177.1 15.1 %all-to-all-start.2 = ((bf16[16,4,16,400]{3,2,1,0:T(8,128)(2,1)}), bf16[16,4,16,400]{3,2,1,0:T(8,128)(2,1)}, u32[]{:S(2)}, u32[]{:S(2)}) async-start(bf16[16,4,16,400]{3,2,1,0:T(8,128)(2,1)} %bitcast.55), calls=%async_computation.2 | async-start | bytes 2097152 | tf_op jit(solution)/shard_map/all_to_all | solution.py:107
  198.6 3.2 collective-permute-start.11
  201.9 41.1 %all-to-all-done.2 = bf16[16,4,16,400]{3,2,1,0:T(8,128)(2,1)} async-done(((bf16[16,4,16,400]{3,2,1,0:T(8,128)(2,1)}), bf16[16,4,16,400]{3,2,1,0:T(8,128)(2,1)}, u32[]{:S(2)}, u32[]{:S(2)}) %all-to-all-start.2) | async-done | bytes 819232 | tf_op jit(solution)/shard_map/all_to_all | solution.py:107
  246.0 8.8 %all-to-all-start.3 = ((bf16[16,4,16,400]{3,2,1,0:T(8,128)(2,1)}), bf16[16,4,16,400]{3,2,1,0:T(8,128)(2,1)}, u32[]{:S(2)}, u32[]{:S(2)}) async-start(bf16[16,4,16,400]{3,2,1,0:T(8,128)(2,1)} %copy.65), calls=%async_computation.3 | async-start | bytes 2097152 | tf_op jit(solution)/shard_map/all_to_all | solution.py:116
  255.0 4.8 %collective-permute-start.12 = (bf16[512,400]{0,1:T(8,128)(2,1)S(1)}, bf16[512,400]{0,1:T(8,128)(2,1)S(1)}, u32[]{:S(2)}, u32[]{:S(2)}) collective-permute-start(bf16[512,400]{0,1:T(8,128)(2,1)S(1)} %add_convert_fusion.3), channel_id=1, source_target_pairs={{0,4},{1,5},{2,6},{3,7},{4,0},{5,1},{6,2},{7,3},{8,12},{9,13},{10,... | collective-permute-start | bytes 1228808 | tf_op jit(solution)/shard_map/ppermute | solution.py:14
  259.8 8.9 %collective-permute-done.12 = bf16[512,400]{0,1:T(8,128)(2,1)S(1)} collective-permute-done((bf16[512,400]{0,1:T(8,128)(2,1)S(1)}, bf16[512,400]{0,1:T(8,128)(2,1)S(1)}, u32[]{:S(2)}, u32[]{:S(2)}) %collective-permute-start.12) | collective-permute-done | bytes 409632 | tf_op jit(solution)/shard_map/ppermute | solution.py:14
  270.7 34.3 %collective-permute-done.13 = bf16[512,400]{0,1:T(8,128)(2,1)S(1)} collective-permute-done((bf16[512,400]{0,1:T(8,128)(2,1)S(1)}, bf16[512,400]{0,1:T(8,128)(2,1)S(1)}, u32[]{:S(2)}, u32[]{:S(2)}) %collective-permute-start.13) | collective-permute-done | bytes 409632 | tf_op jit(solution)/shard_map/ppermute | solution.py:14
  305.9 4.0 collective-permute-start.14
  314.3 13.7 %collective-permute-done.14 = bf16[512,400]{0,1:T(8,128)(2,1)} collective-permute-done((bf16[512,400]{0,1:T(8,128)(2,1)}, bf16[512,400]{0,1:T(8,128)(2,1)}, u32[]{:S(2)}, u32[]{:S(2)}) %collective-permute-start.14) | collective-permute-done | bytes 409632 | tf_op jit(solution)/shard_map/ppermute | solution.py:14
  329.5 7.7 %scatter_fusion = f32[256,400]{1,0:T(8,128)S(1)} fusion(f32[256,400]{1,0:T(8,128)S(1)} %copy.68, s32[1024]{0:T(1024)S(1)} %bitcast.58, f32[1024,400]{1,0:T(8,128)} %copy.69), kind=kCustom, calls=%fused_computation.3 | custom fusion | flops 409600 | bytes 4919296 | tf_op jit(solution)/shard_map/scatter-add | solution.py:118
  339.7 7.3 %scatter_custom_fusion = f32[256,400]{1,0:T(8,128)S(1)} fusion(s32[1024]{0:T(1024)} %bitcast.61, bf16[1024,400]{1,0:T(8,128)(2,1)} %bitcast.22, f32[]{:T(128)} %constant.3.clone.1), kind=kCustom, calls=%fused_computation.5 | custom fusion | flops 819200 | bytes 1458688 | tf_op jit(solution)/shard_map/scatter-add | solution.py:128
  347.1 4.2 collective-permute-start.5
  351.4 4.3 collective-permute-start.16
  358.9 3.8 collective-permute-done.16
  362.7 6.9 %collective-permute-start.17 = (bf16[256,400]{1,0:T(8,128)(2,1)S(1)}, bf16[256,400]{1,0:T(8,128)(2,1)S(1)}, u32[]{:S(2)}, u32[]{:S(2)}) collective-permute-start(bf16[256,400]{1,0:T(8,128)(2,1)S(1)} %add_convert_fusion.12), channel_id=1, source_target_pairs={{0,128},{32,160},{64,192},{96,224},{128,0},{160,32},{192,64},{224,... | collective-permute-start | bytes 614408 | tf_op jit(solution)/shard_map/ppermute | solution.py:14
  369.7 4.5 %collective-permute-start.7 = (bf16[256,400]{1,0:T(8,128)(2,1)S(1)}, bf16[256,400]{1,0:T(8,128)(2,1)S(1)}, u32[]{:S(2)}, u32[]{:S(2)}) collective-permute-start(bf16[256,400]{1,0:T(8,128)(2,1)S(1)} %add_convert_fusion.17), channel_id=1, source_target_pairs={{0,4},{1,5},{2,6},{3,7},{4,0},{5,1},{6,2},{7,3},{8,12},{9,13},{10,... | collective-permute-start | bytes 614408 | tf_op jit(solution)/shard_map/ppermute | solution.py:14
  374.2 18.2 %collective-permute-done.17 = bf16[256,400]{1,0:T(8,128)(2,1)S(1)} collective-permute-done((bf16[256,400]{1,0:T(8,128)(2,1)S(1)}, bf16[256,400]{1,0:T(8,128)(2,1)S(1)}, u32[]{:S(2)}, u32[]{:S(2)}) %collective-permute-start.17) | collective-permute-done | bytes 204832 | tf_op jit(solution)/shard_map/ppermute | solution.py:14
  392.5 8.5 %collective-permute-start.18 = (bf16[256,400]{1,0:T(8,128)(2,1)S(1)}, bf16[256,400]{1,0:T(8,128)(2,1)S(1)}, u32[]{:S(2)}, u32[]{:S(2)}) collective-permute-start(bf16[256,400]{1,0:T(8,128)(2,1)S(1)} %add_convert_fusion.11), channel_id=1, source_target_pairs={{0,256},{32,288},{64,320},{96,352},{128,384},{160,416},{192,448},{... | collective-permute-start | bytes 614408 | tf_op jit(solution)/shard_map/ppermute | solution.py:14
  403.0 21.8 %collective-permute-done.18 = bf16[256,400]{1,0:T(8,128)(2,1)S(1)} collective-permute-done((bf16[256,400]{1,0:T(8,128)(2,1)S(1)}, bf16[256,400]{1,0:T(8,128)(2,1)S(1)}, u32[]{:S(2)}, u32[]{:S(2)}) %collective-permute-start.18) | collective-permute-done | bytes 204832 | tf_op jit(solution)/shard_map/ppermute | solution.py:14
  430.7 11.6 %collective-permute-done.9 = bf16[256,400]{1,0:T(8,128)(2,1)S(1)} collective-permute-done((bf16[256,400]{1,0:T(8,128)(2,1)S(1)}, bf16[256,400]{1,0:T(8,128)(2,1)S(1)}, u32[]{:S(2)}, u32[]{:S(2)}) %collective-permute-start.9) | collective-permute-done | bytes 204832 | tf_op jit(solution)/shard_map/ppermute | solution.py:14
  (92 shorter events, 60.8 us)
Async XLA Ops:
  0.6 70.3 %copy-start = (bf16[4,400,400]{2,1,0:T(8,128)(2,1)S(1)}, bf16[4,400,400]{2,1,0:T(8,128)(2,1)}, u32[]{:S(2)}) copy-start(bf16[4,400,400]{2,1,0:T(8,128)(2,1)} %param.7) | copy-start | bytes 3840004
  7.6 18.3 %copy-start.7 = (s32[1,2]{1,0:T(1,128)S(1)}, s32[1,2]{1,0:T(1,128)}, u32[]{:S(2)}) copy-start(s32[1,2]{1,0:T(1,128)} %param.13) | copy-start | bytes 28
  7.6 20.2 %copy-start.5 = (bf16[256,400]{0,1:T(8,128)(2,1)S(1)}, bf16[256,400]{0,1:T(8,128)(2,1)}, u32[]{:S(2)}) copy-start(bf16[256,400]{0,1:T(8,128)(2,1)} %param.9) | copy-start | bytes 614404
  7.6 63.3 %all-to-all-start = ((bf16[16,4,16,400]{3,2,1,0:T(8,128)(2,1)}), bf16[16,4,16,400]{3,2,1,0:T(8,128)(2,1)S(1)}, u32[]{:S(2)}, u32[]{:S(2)}) async-start(bf16[16,4,16,400]{3,2,1,0:T(8,128)(2,1)} %bitcast.2), calls=%async_computation | async-start | bytes 2097152 | tf_op jit(solution)/shard_map/all_to_all | solution.py:93
  28.7 59.7 %collective-permute-start = (bf16[2,256,400]{1,2,0:T(8,128)(2,1)}, bf16[2,256,400]{1,2,0:T(8,128)(2,1)S(1)}, u32[]{:S(2)}, u32[]{:S(2)}) collective-permute-start(bf16[2,256,400]{1,2,0:T(8,128)(2,1)} %pad_maximum_fusion), channel_id=1, source_target_pairs={{0,1},{1,0},{2,3},{3,2},{4,5},{5,4},{6,7},{7,6},{8,9},{9,8},{10,11... | collective-permute-start | bytes 1228808 | tf_op jit(solution)/shard_map/ppermute | solution.py:14
  71.0 1.8 copy-start.3
  72.7 95.4 %all-to-all-start.1 = ((bf16[16,4,16,400]{3,2,1,0:T(8,128)(2,1)}), bf16[16,4,16,400]{3,2,1,0:T(8,128)(2,1)S(1)}, u32[]{:S(2)}, u32[]{:S(2)}) async-start(bf16[16,4,16,400]{3,2,1,0:T(8,128)(2,1)} %copy.56), calls=%async_computation.1 | async-start | bytes 2097152 | tf_op jit(solution)/shard_map/all_to_all | solution.py:97
  88.4 27.8 %copy-start.8 = (s32[1,1,64]{2,1,0:T(1,128)S(1)}, s32[1,1,64]{2,1,0:T(1,128)}, u32[]{:S(2)}) copy-start(s32[1,1,64]{2,1,0:T(1,128)} %param.12) | copy-start | bytes 772
  88.5 59.0 %copy-start.6 = (s32[1,1,1024]{2,1,0:T(1,128)S(1)}, s32[1,1,1024]{2,1,0:T(1,128)}, u32[]{:S(2)}) copy-start(s32[1,1,1024]{2,1,0:T(1,128)} %param.11) | copy-start | bytes 12292
  88.5 11.7 %collective-permute-start.1 = (bf16[2,256,400]{1,2,0:T(8,128)(2,1)S(1)}, bf16[2,256,400]{1,2,0:T(8,128)(2,1)S(1)}, u32[]{:S(2)}, u32[]{:S(2)}) collective-permute-start(bf16[2,256,400]{1,2,0:T(8,128)(2,1)S(1)} %add_convert_fusion.9), channel_id=1, source_target_pairs={{0,2},{1,3},{2,0},{3,1},{4,6},{5,7},{6,4},{7,5},{8,10},{9,11},{10,... | collective-permute-start | bytes 1228808 | tf_op jit(solution)/shard_map/ppermute | solution.py:14
  100.4 12.3 %collective-permute-start.2 = (bf16[2,256,400]{1,2,0:T(8,128)(2,1)S(1)}, bf16[2,256,400]{1,2,0:T(8,128)(2,1)S(1)}, u32[]{:S(2)}, u32[]{:S(2)}) collective-permute-start(bf16[2,256,400]{1,2,0:T(8,128)(2,1)S(1)} %add_convert_fusion.8), channel_id=1, source_target_pairs={{0,4},{1,5},{2,6},{3,7},{4,0},{5,1},{6,2},{7,3},{8,12},{9,13},{10,... | collective-permute-start | bytes 1228808 | tf_op jit(solution)/shard_map/ppermute | solution.py:14
  112.8 29.6 %collective-permute-start.3 = (bf16[2,256,400]{1,2,0:T(8,128)(2,1)S(1)}, bf16[2,256,400]{1,2,0:T(8,128)(2,1)}, u32[]{:S(2)}, u32[]{:S(2)}) collective-permute-start(bf16[2,256,400]{1,2,0:T(8,128)(2,1)S(1)} %add_convert_fusion.7), channel_id=1, source_target_pairs={{0,8},{1,9},{2,10},{3,11},{4,12},{5,13},{6,14},{7,15},{8,0},{9,1},... | collective-permute-start | bytes 1228808 | tf_op jit(solution)/shard_map/ppermute | solution.py:14
  144.3 21.8 %collective-permute-start.4 = (bf16[2,256,400]{1,2,0:T(8,128)(2,1)}, bf16[2,256,400]{1,2,0:T(8,128)(2,1)}, u32[]{:S(2)}, u32[]{:S(2)}) collective-permute-start(bf16[2,256,400]{1,2,0:T(8,128)(2,1)} %add_convert_fusion.6), channel_id=1, source_target_pairs={{0,16},{1,17},{2,18},{3,19},{4,20},{5,21},{6,22},{7,23},{8,24},{9,... | collective-permute-start | bytes 1228808 | tf_op jit(solution)/shard_map/ppermute | solution.py:14
  170.1 3.2 copy-start.2
  171.9 1.3 copy-start.1
  177.1 65.9 %all-to-all-start.2 = ((bf16[16,4,16,400]{3,2,1,0:T(8,128)(2,1)}), bf16[16,4,16,400]{3,2,1,0:T(8,128)(2,1)}, u32[]{:S(2)}, u32[]{:S(2)}) async-start(bf16[16,4,16,400]{3,2,1,0:T(8,128)(2,1)} %bitcast.55), calls=%async_computation.2 | async-start | bytes 2097152 | tf_op jit(solution)/shard_map/all_to_all | solution.py:107
  194.5 4.0 collective-permute-start.10
  198.6 56.2 %collective-permute-start.11 = (bf16[512,400]{0,1:T(8,128)(2,1)S(1)}, bf16[512,400]{0,1:T(8,128)(2,1)S(1)}, u32[]{:S(2)}, u32[]{:S(2)}) collective-permute-start(bf16[512,400]{0,1:T(8,128)(2,1)S(1)} %add_convert_fusion.4), channel_id=1, source_target_pairs={{0,2},{1,3},{2,0},{3,1},{4,6},{5,7},{6,4},{7,5},{8,10},{9,11},{10,... | collective-permute-start | bytes 1228808 | tf_op jit(solution)/shard_map/ppermute | solution.py:14
  246.0 93.7 %all-to-all-start.3 = ((bf16[16,4,16,400]{3,2,1,0:T(8,128)(2,1)}), bf16[16,4,16,400]{3,2,1,0:T(8,128)(2,1)}, u32[]{:S(2)}, u32[]{:S(2)}) async-start(bf16[16,4,16,400]{3,2,1,0:T(8,128)(2,1)} %copy.65), calls=%async_computation.3 | async-start | bytes 2097152 | tf_op jit(solution)/shard_map/all_to_all | solution.py:116
  255.0 13.7 %collective-permute-start.12 = (bf16[512,400]{0,1:T(8,128)(2,1)S(1)}, bf16[512,400]{0,1:T(8,128)(2,1)S(1)}, u32[]{:S(2)}, u32[]{:S(2)}) collective-permute-start(bf16[512,400]{0,1:T(8,128)(2,1)S(1)} %add_convert_fusion.3), channel_id=1, source_target_pairs={{0,4},{1,5},{2,6},{3,7},{4,0},{5,1},{6,2},{7,3},{8,12},{9,13},{10,... | collective-permute-start | bytes 1228808 | tf_op jit(solution)/shard_map/ppermute | solution.py:14
  268.8 36.2 %collective-permute-start.13 = (bf16[512,400]{0,1:T(8,128)(2,1)S(1)}, bf16[512,400]{0,1:T(8,128)(2,1)S(1)}, u32[]{:S(2)}, u32[]{:S(2)}) collective-permute-start(bf16[512,400]{0,1:T(8,128)(2,1)S(1)} %add_convert_fusion.2), channel_id=1, source_target_pairs={{0,8},{1,9},{2,10},{3,11},{4,12},{5,13},{6,14},{7,15},{8,0},{9,1},... | collective-permute-start | bytes 1228808 | tf_op jit(solution)/shard_map/ppermute | solution.py:14
  305.9 22.1 %collective-permute-start.14 = (bf16[512,400]{0,1:T(8,128)(2,1)}, bf16[512,400]{0,1:T(8,128)(2,1)}, u32[]{:S(2)}, u32[]{:S(2)}) collective-permute-start(bf16[512,400]{0,1:T(8,128)(2,1)} %add_convert_fusion.1), channel_id=1, source_target_pairs={{0,16},{1,17},{2,18},{3,19},{4,20},{5,21},{6,22},{7,23},{8,24},{9,... | collective-permute-start | bytes 1228808 | tf_op jit(solution)/shard_map/ppermute | solution.py:14
  337.2 14.1 %collective-permute-start.15 = (bf16[256,400]{1,0:T(8,128)(2,1)S(1)}, bf16[256,400]{1,0:T(8,128)(2,1)S(1)}, u32[]{:S(2)}, u32[]{:S(2)}) collective-permute-start(bf16[256,400]{1,0:T(8,128)(2,1)S(1)} %convert_element_type.291), channel_id=1, source_target_pairs={{0,32},{32,0},{64,96},{96,64},{128,160},{160,128},{192,224},{224,1... | collective-permute-start | bytes 614408 | tf_op jit(solution)/shard_map/ppermute | solution.py:14
  347.1 8.6 %collective-permute-start.5 = (bf16[256,400]{1,0:T(8,128)(2,1)S(1)}, bf16[256,400]{1,0:T(8,128)(2,1)S(1)}, u32[]{:S(2)}, u32[]{:S(2)}) collective-permute-start(bf16[256,400]{1,0:T(8,128)(2,1)S(1)} %convert_element_type.259), channel_id=1, source_target_pairs={{0,1},{1,0},{2,3},{3,2},{4,5},{5,4},{6,7},{7,6},{8,9},{9,8},{10,11... | collective-permute-start | bytes 614408 | tf_op jit(solution)/shard_map/ppermute | solution.py:14
  351.4 11.2 %collective-permute-start.16 = (bf16[256,400]{1,0:T(8,128)(2,1)S(1)}, bf16[256,400]{1,0:T(8,128)(2,1)S(1)}, u32[]{:S(2)}, u32[]{:S(2)}) collective-permute-start(bf16[256,400]{1,0:T(8,128)(2,1)S(1)} %add_convert_fusion.13), channel_id=1, source_target_pairs={{0,64},{32,96},{64,0},{96,32},{128,192},{160,224},{192,128},{224,1... | collective-permute-start | bytes 614408 | tf_op jit(solution)/shard_map/ppermute | solution.py:14
  355.8 13.8 %collective-permute-start.6 = (bf16[256,400]{1,0:T(8,128)(2,1)S(1)}, bf16[256,400]{1,0:T(8,128)(2,1)S(1)}, u32[]{:S(2)}, u32[]{:S(2)}) collective-permute-start(bf16[256,400]{1,0:T(8,128)(2,1)S(1)} %add_convert_fusion.18), channel_id=1, source_target_pairs={{0,2},{1,3},{2,0},{3,1},{4,6},{5,7},{6,4},{7,5},{8,10},{9,11},{10,... | collective-permute-start | bytes 614408 | tf_op jit(solution)/shard_map/ppermute | solution.py:14
  362.7 65.0 %copy-start.4 = (bf16[16,4,16,400]{3,2,1,0:T(8,128)(2,1)S(1)}, bf16[16,4,16,400]{3,2,1,0:T(8,128)(2,1)}, u32[]{:S(2)}) copy-start(bf16[16,4,16,400]{3,2,1,0:T(8,128)(2,1)} %copy-done.3) | copy-start | bytes 2457604
  362.7 29.7 %collective-permute-start.17 = (bf16[256,400]{1,0:T(8,128)(2,1)S(1)}, bf16[256,400]{1,0:T(8,128)(2,1)S(1)}, u32[]{:S(2)}, u32[]{:S(2)}) collective-permute-start(bf16[256,400]{1,0:T(8,128)(2,1)S(1)} %add_convert_fusion.12), channel_id=1, source_target_pairs={{0,128},{32,160},{64,192},{96,224},{128,0},{160,32},{192,64},{224,... | collective-permute-start | bytes 614408 | tf_op jit(solution)/shard_map/ppermute | solution.py:14
  369.7 31.3 %collective-permute-start.7 = (bf16[256,400]{1,0:T(8,128)(2,1)S(1)}, bf16[256,400]{1,0:T(8,128)(2,1)S(1)}, u32[]{:S(2)}, u32[]{:S(2)}) collective-permute-start(bf16[256,400]{1,0:T(8,128)(2,1)S(1)} %add_convert_fusion.17), channel_id=1, source_target_pairs={{0,4},{1,5},{2,6},{3,7},{4,0},{5,1},{6,2},{7,3},{8,12},{9,13},{10,... | collective-permute-start | bytes 614408 | tf_op jit(solution)/shard_map/ppermute | solution.py:14
  392.5 32.3 %collective-permute-start.18 = (bf16[256,400]{1,0:T(8,128)(2,1)S(1)}, bf16[256,400]{1,0:T(8,128)(2,1)S(1)}, u32[]{:S(2)}, u32[]{:S(2)}) collective-permute-start(bf16[256,400]{1,0:T(8,128)(2,1)S(1)} %add_convert_fusion.11), channel_id=1, source_target_pairs={{0,256},{32,288},{64,320},{96,352},{128,384},{160,416},{192,448},{... | collective-permute-start | bytes 614408 | tf_op jit(solution)/shard_map/ppermute | solution.py:14
  401.1 24.6 %collective-permute-start.8 = (bf16[256,400]{1,0:T(8,128)(2,1)S(1)}, bf16[256,400]{1,0:T(8,128)(2,1)S(1)}, u32[]{:S(2)}, u32[]{:S(2)}) collective-permute-start(bf16[256,400]{1,0:T(8,128)(2,1)S(1)} %add_convert_fusion.16), channel_id=1, source_target_pairs={{0,8},{1,9},{2,10},{3,11},{4,12},{5,13},{6,14},{7,15},{8,0},{9,1},... | collective-permute-start | bytes 614408 | tf_op jit(solution)/shard_map/ppermute | solution.py:14
  425.7 16.6 %collective-permute-start.9 = (bf16[256,400]{1,0:T(8,128)(2,1)S(1)}, bf16[256,400]{1,0:T(8,128)(2,1)S(1)}, u32[]{:S(2)}, u32[]{:S(2)}) collective-permute-start(bf16[256,400]{1,0:T(8,128)(2,1)S(1)} %add_convert_fusion.15), channel_id=1, source_target_pairs={{0,16},{1,17},{2,18},{3,19},{4,20},{5,21},{6,22},{7,23},{8,24},{9,... | collective-permute-start | bytes 614408 | tf_op jit(solution)/shard_map/ppermute | solution.py:14

commit v4 on v3

--- a/solution.py
+++ b/solution.py
@@ -18,42 +18,6 @@
 
 def axis_bits(n):
     return [1 << b for b in range(n.bit_length() - 1)]
-
-
-def group_round(x, axis, stride, size):
-    n = lax.axis_size(axis)
-    me = lax.axis_index(axis)
-    member = (me // stride) % size
-    low = x.astype(BF16)
-    got = [low]
-    for shift in range(1, size):
-        perm = []
-        for i in range(n):
-            m = (i // stride) % size
-            perm.append((i, i + (((m + shift) % size) - m) * stride))
-        got.append(lax.ppermute(low, axis, perm))
-    stacked = jnp.stack(got)
-    order = (member - jnp.arange(size)) % size
-    ordered = stacked[order].astype(F32)
-    total = ordered[0]
-    for j in range(1, size):
-        total = total + ordered[j]
-    return total
-
-
-def sub_axes(n):
-    shapes = {32: ((1, 2), (2, 4), (8, 4)), 16: ((1, 4), (4, 4))}
-    return shapes.get(n)
-
-
-def axis_sum(x, axis):
-    n = lax.axis_size(axis)
-    parts = sub_axes(n)
-    if parts is None:
-        return butterfly_sum(x, axis, axis_bits(n))
-    for stride, size in parts:
-        x = group_round(x, axis, stride, size)
-    return x
 
 
 def softmax_grads(z, y, negs, live):
@@ -115,8 +79,11 @@
     ).astype(BF16)
     back_rows = lax.all_to_all(back_rows, "src", 0, 0, tiled=True)
 
-    dst_local = jax.ops.segment_sum(
-        g_pos[:, None] * z_b.astype(F32), ids_dst, num_segments=part
+    rows = jnp.arange(part, dtype=jnp.int32)[:, None]
+    to_dst = jnp.where(ids_dst[None, :] == rows, g_pos[None, :], 0.0)
+    dst_local = jnp.dot(
+        to_dst, z_b.astype(F32), precision=lax.Precision.HIGHEST,
+        preferred_element_type=F32,
     )
     span_grad = jnp.einsum("bn,bd->nd", g_neg, z_b, preferred_element_type=F32)
     span_sum = butterfly_sum(span_grad, "dst", dst_bits)
@@ -125,8 +92,9 @@
         dst_local = dst_local + jnp.where(spans[index] == own_dst, piece, 0.0)
     grad_dst = butterfly_sum(dst_local, "src", axis_bits(n_src)).astype(BF16)
 
-    src_local = jax.ops.segment_sum(
-        back_rows.reshape(slots, width).astype(F32), ids_src, num_segments=part
+    to_src = (ids_src[None, :] == rows).astype(BF16)
+    src_local = jnp.dot(
+        to_src, back_rows.reshape(slots, width), preferred_element_type=F32
     )
     grad_src = butterfly_sum(src_local, "dst", dst_bits).astype(BF16)
     return (grad_rel, grad_src, grad_dst)

time: 445 us -> 414 us (0.930)
  other arithmetic: 26.9 us -> 9.79 us
  waiting for transfers between devices: 247 us -> 238 us
  local copies, waits for them, and re-layouts: 27.2 us -> 22.3 us
    scatter-add x2 -> x0, other arithmetic: 15 us -> none  [the longest x1 7.66 us: body(): jax.ops.segment_sum(g_pos[:, None] * z_b.astype(F32), ids_dst, num_segmen...]
    ppermute x19, waiting for transfers between devices: 166 us -> 153 us  [butterfly_sum(): other = lax.ppermute(low, axis, [(i, i ^ bit) for i in range(n)])]
    all_to_all x1, waiting for transfers between devices: 41.1 us -> 45.8 us  [body(): lax.all_to_all(upstream.reshape(n_src, rk, cap, width), 'src', 0, 0, tile...]
  transfers between devices with their start and end apart: 23 -> 23, of which waited for: 14 -> 16; matrix products, arithmetic and copies ran while one was open for 11% -> 7% of each run, Pallas kernels for 0% -> 0%
where the time goes in v4:
time: 414 us; the launch traced here: 413 us
  waiting for transfers between devices  238 us (57%)
  starting transfers between devices  125 us (30%)
  local copies, waits for them, and re-layouts  22.3 us (5%)
  matrix products  14.4 us (3%)
  other arithmetic  9.79 us (2%)
    ppermute x19, waiting for transfers between devices, butterfly_sum(): other = lax.ppermute(low, axis, [(i, i ^ bit) for i in range(n)])  153 us
    ppermute x19, starting transfers between devices, butterfly_sum(): other = lax.ppermute(low, axis, [(i, i ^ bit) for i in range(n)])  67.2 us
    all_to_all x1, waiting for transfers between devices, body(): lax.all_to_all(upstream.reshape(n_src, rk, cap, width), 'src', 0, 0, tile...  45.8 us
    all_to_all x1, waiting for transfers between devices, body(): x_in = lax.all_to_all(inputs, 'src', 0, 0, tiled=True)  39.4 us
    all_to_all x1, starting transfers between devices, body(): x_in = lax.all_to_all(inputs, 'src', 0, 0, tiled=True)  18.3 us
    all_to_all x1, starting transfers between devices, body(): z_b = lax.all_to_all(mapped, 'src', 0, 0, tiled=True).reshape(slots, width)  15.6 us
    all_to_all x1, starting transfers between devices, body(): lax.all_to_all(upstream.reshape(n_src, rk, cap, width), 'src', 0, 0, tile...  15.2 us
    all_to_all x1, starting transfers between devices, body(): back_rows = lax.all_to_all(back_rows, 'src', 0, 0, tiled=True)  8.82 us
  transfers between devices with their start and end apart: 23, of which 16 were waited for; matrix products, arithmetic and copies ran while one was open for 7% of the time, Pallas kernels for 0%

profile of v4, /device:TPU:1, one launch (start us, length us, event | category | flops | bytes accessed | tf_op | source)
XLA Modules:
  0.0 412.5 jit_solution(11194310670326296180)
XLA Ops:
  2.5 5.1 %gather_fusion = bf16[1024,400]{1,0:T(8,128)(2,1)} fusion(bf16[256,400]{1,0:T(8,128)(2,1)S(1)} %copy.42, s32[1024]{0:T(1024)S(1)} %broadcast_clamp_fusion.1), kind=kCustom, calls=%fused_computation | custom fusion | bytes 1642496 | tf_op jit(solution)/shard_map/gather | solution.py:56
  7.6 18.3 %all-to-all-start = ((bf16[16,4,16,400]{3,2,1,0:T(8,128)(2,1)}), bf16[16,4,16,400]{3,2,1,0:T(8,128)(2,1)S(1)}, u32[]{:S(2)}, u32[]{:S(2)}) async-start(bf16[16,4,16,400]{3,2,1,0:T(8,128)(2,1)} %bitcast.2), calls=%async_computation | async-start | bytes 2097152 | tf_op jit(solution)/shard_map/all_to_all | solution.py:57
  28.7 2.9 collective-permute-start
  31.6 39.4 %all-to-all-done = bf16[16,4,16,400]{3,2,1,0:T(8,128)(2,1)S(1)} async-done(((bf16[16,4,16,400]{3,2,1,0:T(8,128)(2,1)}), bf16[16,4,16,400]{3,2,1,0:T(8,128)(2,1)S(1)}, u32[]{:S(2)}, u32[]{:S(2)}) %all-to-all-start) | async-done | bytes 819232 | tf_op jit(solution)/shard_map/all_to_all | solution.py:57
  72.7 15.6 %all-to-all-start.1 = ((bf16[16,4,16,400]{3,2,1,0:T(8,128)(2,1)}), bf16[16,4,16,400]{3,2,1,0:T(8,128)(2,1)S(1)}, u32[]{:S(2)}, u32[]{:S(2)}) async-start(bf16[16,4,16,400]{3,2,1,0:T(8,128)(2,1)} %copy.44), calls=%async_computation.1 | async-start | bytes 2097152 | tf_op jit(solution)/shard_map/all_to_all | solution.py:61
  88.5 3.2 collective-permute-start.1
  91.7 8.5 %collective-permute-done.1 = bf16[2,256,400]{1,2,0:T(8,128)(2,1)S(1)} collective-permute-done((bf16[2,256,400]{1,2,0:T(8,128)(2,1)S(1)}, bf16[2,256,400]{1,2,0:T(8,128)(2,1)S(1)}, u32[]{:S(2)}, u32[]{:S(2)}) %collective-permute-start.1) | collective-permute-done | bytes 409632 | tf_op jit(solution)/shard_map/ppermute | solution.py:14
  100.4 4.8 %collective-permute-start.2 = (bf16[2,256,400]{1,2,0:T(8,128)(2,1)S(1)}, bf16[2,256,400]{1,2,0:T(8,128)(2,1)S(1)}, u32[]{:S(2)}, u32[]{:S(2)}) collective-permute-start(bf16[2,256,400]{1,2,0:T(8,128)(2,1)S(1)} %add_convert_fusion.8), channel_id=1, source_target_pairs={{0,4},{1,5},{2,6},{3,7},{4,0},{5,1},{6,2},{7,3},{8,12},{9,13},{10,... | collective-permute-start | bytes 1228808 | tf_op jit(solution)/shard_map/ppermute | solution.py:14
  105.2 7.5 %collective-permute-done.2 = bf16[2,256,400]{1,2,0:T(8,128)(2,1)S(1)} collective-permute-done((bf16[2,256,400]{1,2,0:T(8,128)(2,1)S(1)}, bf16[2,256,400]{1,2,0:T(8,128)(2,1)S(1)}, u32[]{:S(2)}, u32[]{:S(2)}) %collective-permute-start.2) | collective-permute-done | bytes 409632 | tf_op jit(solution)/shard_map/ppermute | solution.py:14
  116.4 26.0 %collective-permute-done.3 = bf16[2,256,400]{1,2,0:T(8,128)(2,1)} collective-permute-done((bf16[2,256,400]{1,2,0:T(8,128)(2,1)S(1)}, bf16[2,256,400]{1,2,0:T(8,128)(2,1)}, u32[]{:S(2)}, u32[]{:S(2)}) %collective-permute-start.3) | collective-permute-done | bytes 409632 | tf_op jit(solution)/shard_map/ppermute | solution.py:14
  144.3 3.3 collective-permute-start.4
  147.6 5.1 %gather_fusion.1 = bf16[1024,400]{1,0:T(8,128)(2,1)} fusion(bf16[256,400]{1,0:T(8,128)(2,1)S(1)} %copy.45, s32[1024]{0:T(1024)S(1)} %broadcast_clamp_fusion), kind=kCustom, calls=%fused_computation.1 | custom fusion | bytes 1642496 | tf_op jit(solution)/shard_map/gather | solution.py:63
  155.8 10.3 %collective-permute-done.4 = bf16[2,256,400]{1,2,0:T(8,128)(2,1)} collective-permute-done((bf16[2,256,400]{1,2,0:T(8,128)(2,1)}, bf16[2,256,400]{1,2,0:T(8,128)(2,1)}, u32[]{:S(2)}, u32[]{:S(2)}) %collective-permute-start.4) | collective-permute-done | bytes 409632 | tf_op jit(solution)/shard_map/ppermute | solution.py:14
  177.0 15.2 %all-to-all-start.2 = ((bf16[16,4,16,400]{3,2,1,0:T(8,128)(2,1)}), bf16[16,4,16,400]{3,2,1,0:T(8,128)(2,1)}, u32[]{:S(2)}, u32[]{:S(2)}) async-start(bf16[16,4,16,400]{3,2,1,0:T(8,128)(2,1)} %bitcast.56), calls=%async_computation.2 | async-start | bytes 2097152 | tf_op jit(solution)/shard_map/all_to_all | solution.py:71
  197.2 45.8 %all-to-all-done.2 = bf16[16,4,16,400]{3,2,1,0:T(8,128)(2,1)} async-done(((bf16[16,4,16,400]{3,2,1,0:T(8,128)(2,1)}), bf16[16,4,16,400]{3,2,1,0:T(8,128)(2,1)}, u32[]{:S(2)}, u32[]{:S(2)}) %all-to-all-start.2) | async-done | bytes 819232 | tf_op jit(solution)/shard_map/all_to_all | solution.py:71
  246.0 8.8 %all-to-all-start.3 = ((bf16[16,4,16,400]{3,2,1,0:T(8,128)(2,1)}), bf16[16,4,16,400]{3,2,1,0:T(8,128)(2,1)}, u32[]{:S(2)}, u32[]{:S(2)}) async-start(bf16[16,4,16,400]{3,2,1,0:T(8,128)(2,1)} %copy.53), calls=%async_computation.3 | async-start | bytes 2097152 | tf_op jit(solution)/shard_map/all_to_all | solution.py:80
  254.9 3.2 collective-permute-start.11
  258.1 9.1 %collective-permute-done.11 = bf16[512,400]{0,1:T(8,128)(2,1)S(1)} collective-permute-done((bf16[512,400]{0,1:T(8,128)(2,1)S(1)}, bf16[512,400]{0,1:T(8,128)(2,1)S(1)}, u32[]{:S(2)}, u32[]{:S(2)}) %collective-permute-start.11) | collective-permute-done | bytes 409632 | tf_op jit(solution)/shard_map/ppermute | solution.py:14
  267.3 4.9 %collective-permute-start.12 = (bf16[512,400]{0,1:T(8,128)(2,1)S(1)}, bf16[512,400]{0,1:T(8,128)(2,1)S(1)}, u32[]{:S(2)}, u32[]{:S(2)}) collective-permute-start(bf16[512,400]{0,1:T(8,128)(2,1)S(1)} %add_convert_fusion.3), channel_id=1, source_target_pairs={{0,4},{1,5},{2,6},{3,7},{4,0},{5,1},{6,2},{7,3},{8,12},{9,13},{10,... | collective-permute-start | bytes 1228808 | tf_op jit(solution)/shard_map/ppermute | solution.py:14
  272.2 8.1 %collective-permute-done.12 = bf16[512,400]{0,1:T(8,128)(2,1)S(1)} collective-permute-done((bf16[512,400]{0,1:T(8,128)(2,1)S(1)}, bf16[512,400]{0,1:T(8,128)(2,1)S(1)}, u32[]{:S(2)}, u32[]{:S(2)}) %collective-permute-start.12) | collective-permute-done | bytes 409632 | tf_op jit(solution)/shard_map/ppermute | solution.py:14
  282.3 24.4 %collective-permute-done.13 = bf16[512,400]{0,1:T(8,128)(2,1)S(1)} collective-permute-done((bf16[512,400]{0,1:T(8,128)(2,1)S(1)}, bf16[512,400]{0,1:T(8,128)(2,1)S(1)}, u32[]{:S(2)}, u32[]{:S(2)}) %collective-permute-start.13) | collective-permute-done | bytes 409632 | tf_op jit(solution)/shard_map/ppermute | solution.py:14
  309.1 20.3 %collective-permute-done.14 = bf16[512,400]{0,1:T(8,128)(2,1)S(1)} collective-permute-done((bf16[512,400]{0,1:T(8,128)(2,1)S(1)}, bf16[512,400]{0,1:T(8,128)(2,1)S(1)}, u32[]{:S(2)}, u32[]{:S(2)}) %collective-permute-start.14) | collective-permute-done | bytes 409632 | tf_op jit(solution)/shard_map/ppermute | solution.py:14
  330.9 3.1 collective-permute-start.15
  339.0 4.6 %collective-permute-start.16 = (bf16[256,400]{0,1:T(8,128)(2,1)S(1)}, bf16[256,400]{0,1:T(8,128)(2,1)S(1)}, u32[]{:S(2)}, u32[]{:S(2)}) collective-permute-start(bf16[256,400]{0,1:T(8,128)(2,1)S(1)} %add_convert_fusion.13), channel_id=1, source_target_pairs={{0,64},{32,96},{64,0},{96,32},{128,192},{160,224},{192,128},{224,1... | collective-permute-start | bytes 614408 | tf_op jit(solution)/shard_map/ppermute | solution.py:14
  343.7 3.3 collective-permute-start.6
  347.9 6.3 %collective-permute-start.17 = (bf16[256,400]{0,1:T(8,128)(2,1)S(1)}, bf16[256,400]{0,1:T(8,128)(2,1)S(1)}, u32[]{:S(2)}, u32[]{:S(2)}) collective-permute-start(bf16[256,400]{0,1:T(8,128)(2,1)S(1)} %add_convert_fusion.12), channel_id=1, source_target_pairs={{0,128},{32,160},{64,192},{96,224},{128,0},{160,32},{192,64},{224,... | collective-permute-start | bytes 614408 | tf_op jit(solution)/shard_map/ppermute | solution.py:14
  354.2 4.8 %collective-permute-start.7 = (bf16[256,400]{0,1:T(8,128)(2,1)S(1)}, bf16[256,400]{0,1:T(8,128)(2,1)S(1)}, u32[]{:S(2)}, u32[]{:S(2)}) collective-permute-start(bf16[256,400]{0,1:T(8,128)(2,1)S(1)} %add_convert_fusion.17), channel_id=1, source_target_pairs={{0,4},{1,5},{2,6},{3,7},{4,0},{5,1},{6,2},{7,3},{8,12},{9,13},{10,... | collective-permute-start | bytes 614408 | tf_op jit(solution)/shard_map/ppermute | solution.py:14
  359.0 13.4 %collective-permute-done.17 = bf16[256,400]{0,1:T(8,128)(2,1)S(1)} collective-permute-done((bf16[256,400]{0,1:T(8,128)(2,1)S(1)}, bf16[256,400]{0,1:T(8,128)(2,1)S(1)}, u32[]{:S(2)}, u32[]{:S(2)}) %collective-permute-start.17) | collective-permute-done | bytes 204832 | tf_op jit(solution)/shard_map/ppermute | solution.py:14
  372.4 7.3 %collective-permute-start.18 = (bf16[256,400]{0,1:T(8,128)(2,1)S(1)}, bf16[256,400]{0,1:T(8,128)(2,1)S(1)}, u32[]{:S(2)}, u32[]{:S(2)}) collective-permute-start(bf16[256,400]{0,1:T(8,128)(2,1)S(1)} %add_convert_fusion.11), channel_id=1, source_target_pairs={{0,256},{32,288},{64,320},{96,352},{128,384},{160,416},{192,448},{... | collective-permute-start | bytes 614408 | tf_op jit(solution)/shard_map/ppermute | solution.py:14
  381.8 15.9 %collective-permute-done.18 = bf16[256,400]{0,1:T(8,128)(2,1)S(1)} collective-permute-done((bf16[256,400]{0,1:T(8,128)(2,1)S(1)}, bf16[256,400]{0,1:T(8,128)(2,1)S(1)}, u32[]{:S(2)}, u32[]{:S(2)}) %collective-permute-start.18) | collective-permute-done | bytes 204832 | tf_op jit(solution)/shard_map/ppermute | solution.py:14
  400.5 3.0 bitcast_convert_fusion
  403.5 8.3 %collective-permute-done.9 = bf16[256,400]{0,1:T(8,128)(2,1)S(1)} collective-permute-done((bf16[256,400]{0,1:T(8,128)(2,1)S(1)}, bf16[256,400]{0,1:T(8,128)(2,1)S(1)}, u32[]{:S(2)}, u32[]{:S(2)}) %collective-permute-start.9) | collective-permute-done | bytes 204832 | tf_op jit(solution)/shard_map/ppermute | solution.py:14
  (85 shorter events, 50.4 us)
Async XLA Ops:
  0.6 70.3 %copy-start = (bf16[4,400,400]{2,1,0:T(8,128)(2,1)S(1)}, bf16[4,400,400]{2,1,0:T(8,128)(2,1)}, u32[]{:S(2)}) copy-start(bf16[4,400,400]{2,1,0:T(8,128)(2,1)} %param.7) | copy-start | bytes 3840004
  7.6 18.3 %copy-start.8 = (s32[1,2]{1,0:T(1,128)S(1)}, s32[1,2]{1,0:T(1,128)}, u32[]{:S(2)}) copy-start(s32[1,2]{1,0:T(1,128)} %param.13) | copy-start | bytes 28
  7.6 20.2 %copy-start.5 = (bf16[256,400]{0,1:T(8,128)(2,1)S(1)}, bf16[256,400]{0,1:T(8,128)(2,1)}, u32[]{:S(2)}) copy-start(bf16[256,400]{0,1:T(8,128)(2,1)} %param.9) | copy-start | bytes 614404
  7.6 63.3 %all-to-all-start = ((bf16[16,4,16,400]{3,2,1,0:T(8,128)(2,1)}), bf16[16,4,16,400]{3,2,1,0:T(8,128)(2,1)S(1)}, u32[]{:S(2)}, u32[]{:S(2)}) async-start(bf16[16,4,16,400]{3,2,1,0:T(8,128)(2,1)} %bitcast.2), calls=%async_computation | async-start | bytes 2097152 | tf_op jit(solution)/shard_map/all_to_all | solution.py:57
  28.7 59.7 %collective-permute-start = (bf16[2,256,400]{1,2,0:T(8,128)(2,1)}, bf16[2,256,400]{1,2,0:T(8,128)(2,1)S(1)}, u32[]{:S(2)}, u32[]{:S(2)}) collective-permute-start(bf16[2,256,400]{1,2,0:T(8,128)(2,1)} %pad_maximum_fusion), channel_id=1, source_target_pairs={{0,1},{1,0},{2,3},{3,2},{4,5},{5,4},{6,7},{7,6},{8,9},{9,8},{10,11... | collective-permute-start | bytes 1228808 | tf_op jit(solution)/shard_map/ppermute | solution.py:14
  71.0 1.8 copy-start.3
  72.7 95.3 %all-to-all-start.1 = ((bf16[16,4,16,400]{3,2,1,0:T(8,128)(2,1)}), bf16[16,4,16,400]{3,2,1,0:T(8,128)(2,1)S(1)}, u32[]{:S(2)}, u32[]{:S(2)}) async-start(bf16[16,4,16,400]{3,2,1,0:T(8,128)(2,1)} %copy.44), calls=%async_computation.1 | async-start | bytes 2097152 | tf_op jit(solution)/shard_map/all_to_all | solution.py:61
  88.4 27.8 %copy-start.9 = (s32[1,1,64]{2,1,0:T(1,128)S(1)}, s32[1,1,64]{2,1,0:T(1,128)}, u32[]{:S(2)}) copy-start(s32[1,1,64]{2,1,0:T(1,128)} %param.12) | copy-start | bytes 772
  88.5 59.0 %copy-start.6 = (s32[1,1,1024]{2,1,0:T(1,128)S(1)}, s32[1,1,1024]{2,1,0:T(1,128)}, u32[]{:S(2)}) copy-start(s32[1,1,1024]{2,1,0:T(1,128)} %param.11) | copy-start | bytes 12292
  88.5 11.7 %collective-permute-start.1 = (bf16[2,256,400]{1,2,0:T(8,128)(2,1)S(1)}, bf16[2,256,400]{1,2,0:T(8,128)(2,1)S(1)}, u32[]{:S(2)}, u32[]{:S(2)}) collective-permute-start(bf16[2,256,400]{1,2,0:T(8,128)(2,1)S(1)} %add_convert_fusion.9), channel_id=1, source_target_pairs={{0,2},{1,3},{2,0},{3,1},{4,6},{5,7},{6,4},{7,5},{8,10},{9,11},{10,... | collective-permute-start | bytes 1228808 | tf_op jit(solution)/shard_map/ppermute | solution.py:14
  100.4 12.3 %collective-permute-start.2 = (bf16[2,256,400]{1,2,0:T(8,128)(2,1)S(1)}, bf16[2,256,400]{1,2,0:T(8,128)(2,1)S(1)}, u32[]{:S(2)}, u32[]{:S(2)}) collective-permute-start(bf16[2,256,400]{1,2,0:T(8,128)(2,1)S(1)} %add_convert_fusion.8), channel_id=1, source_target_pairs={{0,4},{1,5},{2,6},{3,7},{4,0},{5,1},{6,2},{7,3},{8,12},{9,13},{10,... | collective-permute-start | bytes 1228808 | tf_op jit(solution)/shard_map/ppermute | solution.py:14
  112.8 29.6 %collective-permute-start.3 = (bf16[2,256,400]{1,2,0:T(8,128)(2,1)S(1)}, bf16[2,256,400]{1,2,0:T(8,128)(2,1)}, u32[]{:S(2)}, u32[]{:S(2)}) collective-permute-start(bf16[2,256,400]{1,2,0:T(8,128)(2,1)S(1)} %add_convert_fusion.7), channel_id=1, source_target_pairs={{0,8},{1,9},{2,10},{3,11},{4,12},{5,13},{6,14},{7,15},{8,0},{9,1},... | collective-permute-start | bytes 1228808 | tf_op jit(solution)/shard_map/ppermute | solution.py:14
  144.3 21.8 %collective-permute-start.4 = (bf16[2,256,400]{1,2,0:T(8,128)(2,1)}, bf16[2,256,400]{1,2,0:T(8,128)(2,1)}, u32[]{:S(2)}, u32[]{:S(2)}) collective-permute-start(bf16[2,256,400]{1,2,0:T(8,128)(2,1)} %add_convert_fusion.6), channel_id=1, source_target_pairs={{0,16},{1,17},{2,18},{3,19},{4,20},{5,21},{6,22},{7,23},{8,24},{9,... | collective-permute-start | bytes 1228808 | tf_op jit(solution)/shard_map/ppermute | solution.py:14
  170.0 3.2 copy-start.2
  177.0 65.9 %all-to-all-start.2 = ((bf16[16,4,16,400]{3,2,1,0:T(8,128)(2,1)}), bf16[16,4,16,400]{3,2,1,0:T(8,128)(2,1)}, u32[]{:S(2)}, u32[]{:S(2)}) async-start(bf16[16,4,16,400]{3,2,1,0:T(8,128)(2,1)} %bitcast.56), calls=%async_computation.2 | async-start | bytes 2097152 | tf_op jit(solution)/shard_map/all_to_all | solution.py:71
  194.5 60.3 %collective-permute-start.10 = (bf16[512,400]{0,1:T(8,128)(2,1)S(1)}, bf16[512,400]{0,1:T(8,128)(2,1)S(1)}, u32[]{:S(2)}, u32[]{:S(2)}) collective-permute-start(bf16[512,400]{0,1:T(8,128)(2,1)S(1)} %convolution_convert_fusion), channel_id=1, source_target_pairs={{0,1},{1,0},{2,3},{3,2},{4,5},{5,4},{6,7},{7,6},{8,9},{9,8},{10,11... | collective-permute-start | bytes 1228808 | tf_op jit(solution)/shard_map/ppermute | solution.py:14
  246.0 88.0 %all-to-all-start.3 = ((bf16[16,4,16,400]{3,2,1,0:T(8,128)(2,1)}), bf16[16,4,16,400]{3,2,1,0:T(8,128)(2,1)}, u32[]{:S(2)}, u32[]{:S(2)}) async-start(bf16[16,4,16,400]{3,2,1,0:T(8,128)(2,1)} %copy.53), calls=%async_computation.3 | async-start | bytes 2097152 | tf_op jit(solution)/shard_map/all_to_all | solution.py:80
  254.9 12.2 %collective-permute-start.11 = (bf16[512,400]{0,1:T(8,128)(2,1)S(1)}, bf16[512,400]{0,1:T(8,128)(2,1)S(1)}, u32[]{:S(2)}, u32[]{:S(2)}) collective-permute-start(bf16[512,400]{0,1:T(8,128)(2,1)S(1)} %add_convert_fusion.4), channel_id=1, source_target_pairs={{0,2},{1,3},{2,0},{3,1},{4,6},{5,7},{6,4},{7,5},{8,10},{9,11},{10,... | collective-permute-start | bytes 1228808 | tf_op jit(solution)/shard_map/ppermute | solution.py:14
  267.3 13.0 %collective-permute-start.12 = (bf16[512,400]{0,1:T(8,128)(2,1)S(1)}, bf16[512,400]{0,1:T(8,128)(2,1)S(1)}, u32[]{:S(2)}, u32[]{:S(2)}) collective-permute-start(bf16[512,400]{0,1:T(8,128)(2,1)S(1)} %add_convert_fusion.3), channel_id=1, source_target_pairs={{0,4},{1,5},{2,6},{3,7},{4,0},{5,1},{6,2},{7,3},{8,12},{9,13},{10,... | collective-permute-start | bytes 1228808 | tf_op jit(solution)/shard_map/ppermute | solution.py:14
  280.4 26.4 %collective-permute-start.13 = (bf16[512,400]{0,1:T(8,128)(2,1)S(1)}, bf16[512,400]{0,1:T(8,128)(2,1)S(1)}, u32[]{:S(2)}, u32[]{:S(2)}) collective-permute-start(bf16[512,400]{0,1:T(8,128)(2,1)S(1)} %add_convert_fusion.2), channel_id=1, source_target_pairs={{0,8},{1,9},{2,10},{3,11},{4,12},{5,13},{6,14},{7,15},{8,0},{9,1},... | collective-permute-start | bytes 1228808 | tf_op jit(solution)/shard_map/ppermute | solution.py:14
  306.8 27.1 %copy-start.7 = (s32[1,1,1024]{2,1,0:T(1,128)S(1)}, s32[1,1,1024]{2,1,0:T(1,128)}, u32[]{:S(2)}) copy-start(s32[1,1,1024]{2,1,0:T(1,128)} %param.10) | copy-start | bytes 12292
  306.9 22.6 %collective-permute-start.14 = (bf16[512,400]{0,1:T(8,128)(2,1)S(1)}, bf16[512,400]{0,1:T(8,128)(2,1)S(1)}, u32[]{:S(2)}, u32[]{:S(2)}) collective-permute-start(bf16[512,400]{0,1:T(8,128)(2,1)S(1)} %add_convert_fusion.1), channel_id=1, source_target_pairs={{0,16},{1,17},{2,18},{3,19},{4,20},{5,21},{6,22},{7,23},{8,24},{9,... | collective-permute-start | bytes 1228808 | tf_op jit(solution)/shard_map/ppermute | solution.py:14
  330.9 8.0 %collective-permute-start.15 = (bf16[256,400]{0,1:T(8,128)(2,1)S(1)}, bf16[256,400]{0,1:T(8,128)(2,1)S(1)}, u32[]{:S(2)}, u32[]{:S(2)}) collective-permute-start(bf16[256,400]{0,1:T(8,128)(2,1)S(1)} %fusion.27), channel_id=1, source_target_pairs={{0,32},{32,0},{64,96},{96,64},{128,160},{160,128},{192,224},{224,1... | collective-permute-start | bytes 614408 | tf_op jit(solution)/shard_map/ppermute | solution.py:14
  335.8 7.9 %collective-permute-start.5 = (bf16[256,400]{0,1:T(8,128)(2,1)S(1)}, bf16[256,400]{0,1:T(8,128)(2,1)S(1)}, u32[]{:S(2)}, u32[]{:S(2)}) collective-permute-start(bf16[256,400]{0,1:T(8,128)(2,1)S(1)} %convolution_convert_fusion.1), channel_id=1, source_target_pairs={{0,1},{1,0},{2,3},{3,2},{4,5},{5,4},{6,7},{7,6},{8,9},{9,8},{10,11... | collective-permute-start | bytes 614408 | tf_op jit(solution)/shard_map/ppermute | solution.py:14
  339.0 61.5 %copy-start.4 = (bf16[16,4,16,400]{3,2,1,0:T(8,128)(2,1)S(1)}, bf16[16,4,16,400]{3,2,1,0:T(8,128)(2,1)}, u32[]{:S(2)}) copy-start(bf16[16,4,16,400]{3,2,1,0:T(8,128)(2,1)} %copy-done.3) | copy-start | bytes 2457604
  339.0 8.8 %collective-permute-start.16 = (bf16[256,400]{0,1:T(8,128)(2,1)S(1)}, bf16[256,400]{0,1:T(8,128)(2,1)S(1)}, u32[]{:S(2)}, u32[]{:S(2)}) collective-permute-start(bf16[256,400]{0,1:T(8,128)(2,1)S(1)} %add_convert_fusion.13), channel_id=1, source_target_pairs={{0,64},{32,96},{64,0},{96,32},{128,192},{160,224},{192,128},{224,1... | collective-permute-start | bytes 614408 | tf_op jit(solution)/shard_map/ppermute | solution.py:14
  343.7 10.5 %collective-permute-start.6 = (bf16[256,400]{0,1:T(8,128)(2,1)S(1)}, bf16[256,400]{0,1:T(8,128)(2,1)S(1)}, u32[]{:S(2)}, u32[]{:S(2)}) collective-permute-start(bf16[256,400]{0,1:T(8,128)(2,1)S(1)} %add_convert_fusion.18), channel_id=1, source_target_pairs={{0,2},{1,3},{2,0},{3,1},{4,6},{5,7},{6,4},{7,5},{8,10},{9,11},{10,... | collective-permute-start | bytes 614408 | tf_op jit(solution)/shard_map/ppermute | solution.py:14
  347.9 24.5 %collective-permute-start.17 = (bf16[256,400]{0,1:T(8,128)(2,1)S(1)}, bf16[256,400]{0,1:T(8,128)(2,1)S(1)}, u32[]{:S(2)}, u32[]{:S(2)}) collective-permute-start(bf16[256,400]{0,1:T(8,128)(2,1)S(1)} %add_convert_fusion.12), channel_id=1, source_target_pairs={{0,128},{32,160},{64,192},{96,224},{128,0},{160,32},{192,64},{224,... | collective-permute-start | bytes 614408 | tf_op jit(solution)/shard_map/ppermute | solution.py:14
  354.2 25.5 %collective-permute-start.7 = (bf16[256,400]{0,1:T(8,128)(2,1)S(1)}, bf16[256,400]{0,1:T(8,128)(2,1)S(1)}, u32[]{:S(2)}, u32[]{:S(2)}) collective-permute-start(bf16[256,400]{0,1:T(8,128)(2,1)S(1)} %add_convert_fusion.17), channel_id=1, source_target_pairs={{0,4},{1,5},{2,6},{3,7},{4,0},{5,1},{6,2},{7,3},{8,12},{9,13},{10,... | collective-permute-start | bytes 614408 | tf_op jit(solution)/shard_map/ppermute | solution.py:14
  372.4 25.2 %collective-permute-start.18 = (bf16[256,400]{0,1:T(8,128)(2,1)S(1)}, bf16[256,400]{0,1:T(8,128)(2,1)S(1)}, u32[]{:S(2)}, u32[]{:S(2)}) collective-permute-start(bf16[256,400]{0,1:T(8,128)(2,1)S(1)} %add_convert_fusion.11), channel_id=1, source_target_pairs={{0,256},{32,288},{64,320},{96,352},{128,384},{160,416},{192,448},{... | collective-permute-start | bytes 614408 | tf_op jit(solution)/shard_map/ppermute | solution.py:14
  379.8 18.7 %collective-permute-start.8 = (bf16[256,400]{0,1:T(8,128)(2,1)S(1)}, bf16[256,400]{0,1:T(8,128)(2,1)S(1)}, u32[]{:S(2)}, u32[]{:S(2)}) collective-permute-start(bf16[256,400]{0,1:T(8,128)(2,1)S(1)} %add_convert_fusion.16), channel_id=1, source_target_pairs={{0,8},{1,9},{2,10},{3,11},{4,12},{5,13},{6,14},{7,15},{8,0},{9,1},... | collective-permute-start | bytes 614408 | tf_op jit(solution)/shard_map/ppermute | solution.py:14
  398.6 13.2 %collective-permute-start.9 = (bf16[256,400]{0,1:T(8,128)(2,1)S(1)}, bf16[256,400]{0,1:T(8,128)(2,1)S(1)}, u32[]{:S(2)}, u32[]{:S(2)}) collective-permute-start(bf16[256,400]{0,1:T(8,128)(2,1)S(1)} %add_convert_fusion.15), channel_id=1, source_target_pairs={{0,16},{1,17},{2,18},{3,19},{4,20},{5,21},{6,22},{7,23},{8,24},{9,... | collective-permute-start | bytes 614408 | tf_op jit(solution)/shard_map/ppermute | solution.py:14
  (1 other events, 1.4 us)

commit v5 on v4

--- a/solution.py
+++ b/solution.py
@@ -9,11 +9,23 @@
 
 def butterfly_sum(x, axis, bits):
     n = lax.axis_size(axis)
+    shape = x.shape
+    x = lanes(x)
     for bit in bits:
         low = x.astype(BF16)
         other = lax.ppermute(low, axis, [(i, i ^ bit) for i in range(n)])
         x = low.astype(F32) + other.astype(F32)
-    return x
+    return x.reshape(shape)
+
+
+def lanes(x):
+    return x.reshape(-1, 128) if x.size % 128 == 0 else x
+
+
+def exchange(x, axis):
+    shape = x.shape
+    flat = x.reshape(shape[0], -1)
+    return lax.all_to_all(flat, axis, 0, 0, tiled=True).reshape(shape)
 
 
 def axis_bits(n):
@@ -54,11 +66,11 @@
     negs = butterfly_sum(pieces, "dst", dst_bits).astype(BF16).reshape(nch * part, width)
 
     inputs = src_emb[ids_src].reshape(n_src, rk, cap, width)
-    x_in = lax.all_to_all(inputs, "src", 0, 0, tiled=True)
+    x_in = exchange(inputs, "src")
     mapped = jnp.einsum(
         "pkcd,kde->pkce", x_in, rel_ops, preferred_element_type=F32
     ).astype(BF16)
-    z_b = lax.all_to_all(mapped, "src", 0, 0, tiled=True).reshape(slots, width)
+    z_b = exchange(mapped, "src").reshape(slots, width)
 
     y_b = dst_emb[ids_dst]
     lane = jnp.arange(cap, dtype=jnp.int32)
@@ -68,16 +80,14 @@
         g_pos[:, None] * y_b.astype(F32)
         + jnp.dot(g_neg, negs, preferred_element_type=F32)
     ).astype(BF16)
-    u_in = lax.all_to_all(
-        upstream.reshape(n_src, rk, cap, width), "src", 0, 0, tiled=True
-    )
+    u_in = exchange(upstream.reshape(n_src, rk, cap, width), "src")
     grad_rel = jnp.einsum(
         "pkcd,pkce->kde", x_in, u_in, preferred_element_type=F32
     ).astype(BF16)
     back_rows = jnp.einsum(
         "pkce,kde->pkcd", u_in, rel_ops, preferred_element_type=F32
     ).astype(BF16)
-    back_rows = lax.all_to_all(back_rows, "src", 0, 0, tiled=True)
+    back_rows = exchange(back_rows, "src")
 
     rows = jnp.arange(part, dtype=jnp.int32)[:, None]
     to_dst = jnp.where(ids_dst[None, :] == rows, g_pos[None, :], 0.0)

time: 414 us -> 500 us (1.21); the launches traced: 413 us -> 491 us
  local copies, waits for them, and re-layouts: 22.3 us -> 95.3 us
  other arithmetic: 9.79 us -> 61.5 us
  waiting for transfers between devices: 238 us -> 203 us
  starting transfers between devices: 125 us -> 115 us
    all_to_all x0 -> x8, other arithmetic: none -> 49.7 us  [exchange(): return lax.all_to_all(flat, axis, 0, 0, tiled=True).reshape(shape)]
    all_to_all x4, waiting for transfers between devices: 85.2 us -> 35.6 us  [exchange(): return lax.all_to_all(flat, axis, 0, 0, tiled=True).reshape(shape)]
    unnamed x22 -> x34, local copies, waits for them, and re-layouts: 3.17 us -> 27.9 us
    all_to_all x0 -> x5, local copies, waits for them, and re-layouts: none -> 23.1 us  [exchange(): return lax.all_to_all(flat, axis, 0, 0, tiled=True).reshape(shape)]
    ppermute x19, waiting for transfers between devices: 153 us -> 167 us  [butterfly_sum(): other = lax.ppermute(low, axis, [(i, i ^ bit) for i in range(n)])]
    convert_element_type x1 -> x9, local copies, waits for them, and re-layouts: 1.65 us -> 9.22 us  [the longest x6 6.19 us: butterfly_sum(): low = x.astype(BF16)]
    another operation x0 -> x4, local copies, waits for them, and re-layouts: none -> 7.52 us  [the longest x2 3.9 us: body(): z_b = exchange(mapped, 'src').reshape(slots, width)]
    reshape x1 -> x3, local copies, waits for them, and re-layouts: 0.79 us -> 7.78 us  [the longest x2 6.69 us: exchange(): return lax.all_to_all(flat, axis, 0, 0, tiled=True).reshape(shape)]
  transfers between devices with their start and end apart: 23 -> 23, of which waited for: 16 -> 14; matrix products, arithmetic and copies ran while one was open for 7% -> 21% of each run, Pallas kernels for 0% -> 0%
where the time goes in v5:
time: 500 us; the launch traced here: 491 us
  waiting for transfers between devices  203 us (41%)
  starting transfers between devices  115 us (23%)
  local copies, waits for them, and re-layouts  95.3 us (19%)
  other arithmetic  61.5 us (12%)
  matrix products  14.2 us (3%)
    ppermute x19, waiting for transfers between devices, butterfly_sum(): other = lax.ppermute(low, axis, [(i, i ^ bit) for i in range(n)])  167 us
    ppermute x19, starting transfers between devices, butterfly_sum(): other = lax.ppermute(low, axis, [(i, i ^ bit) for i in range(n)])  63.4 us
    all_to_all x4, starting transfers between devices, exchange(): return lax.all_to_all(flat, axis, 0, 0, tiled=True).reshape(shape)  51.1 us
    all_to_all x8, other arithmetic, exchange(): return lax.all_to_all(flat, axis, 0, 0, tiled=True).reshape(shape)  49.7 us
    all_to_all x4, waiting for transfers between devices, exchange(): return lax.all_to_all(flat, axis, 0, 0, tiled=True).reshape(shape)  35.6 us
    unnamed x34, local copies, waits for them, and re-layouts  27.9 us
    all_to_all x5, local copies, waits for them, and re-layouts, exchange(): return lax.all_to_all(flat, axis, 0, 0, tiled=True).reshape(shape)  23.1 us
  transfers between devices with their start and end apart: 23, of which 14 were waited for; matrix products, arithmetic and copies ran while one was open for 21% of the time, Pallas kernels for 0%

profile of v5, /device:TPU:1, one launch (start us, length us, event | category | flops | bytes accessed | tf_op | source)
XLA Modules:
  0.0 490.9 jit_solution(18351528693926529151)
XLA Ops:
  2.5 5.1 %gather_fusion = bf16[1024,400]{1,0:T(8,128)(2,1)} fusion(bf16[256,400]{1,0:T(8,128)(2,1)S(1)} %copy.34, s32[1024]{0:T(1024)S(1)} %broadcast_clamp_fusion.1), kind=kCustom, calls=%fused_computation | custom fusion | bytes 1642496 | tf_op jit(solution)/shard_map/gather | solution.py:68
  7.6 5.0 %all_to_all.32 = bf16[16,1,25600]{2,1,0:T(2,128)(2,1)S(1)} reshape(bf16[1024,400]{1,0:T(8,128)(2,1)} %gather_fusion) | data formatting | bytes 1638400 | tf_op jit(solution)/shard_map/all_to_all | solution.py:28
  13.2 6.5 %reduce.4 = bf16[16,25600]{1,0:T(8,128)(2,1)} reduce(bf16[16,1,25600]{2,1,0:T(2,128)(2,1)S(1)} %all_to_all.32, bf16[]{:T(256)} %broadcast.92), dimensions={1}, to_apply=%all_to_all.32.reduce_sub_computation | reduce | bytes 1638402 | tf_op jit(solution)/shard_map/all_to_all | solution.py:28
  22.4 18.2 %all-to-all-start = ((bf16[16,2,12800]{2,1,0:T(2,128)(2,1)}), bf16[16,2,12800]{2,1,0:T(2,128)(2,1)}, u32[]{:S(2)}, u32[]{:S(2)}) async-start(bf16[16,2,12800]{2,1,0:T(2,128)(2,1)} %reshape.220), calls=%async_computation | async-start | bytes 1638400 | tf_op jit(solution)/shard_map/all_to_all | solution.py:28
  52.4 23.2 %all-to-all-done = bf16[16,2,12800]{2,1,0:T(2,128)(2,1)} async-done(((bf16[16,2,12800]{2,1,0:T(2,128)(2,1)}), bf16[16,2,12800]{2,1,0:T(2,128)(2,1)}, u32[]{:S(2)}, u32[]{:S(2)}) %all-to-all-start) | async-done | bytes 819232 | tf_op jit(solution)/shard_map/all_to_all | solution.py:28
  80.0 5.8 %reduce = bf16[16,25600]{1,0:T(8,128)(2,1)} reduce(bf16[16,1,25600]{2,1,0:T(2,128)(2,1)S(1)} %reshape.221, bf16[]{:T(256)} %constant.24), dimensions={1}, to_apply=%all_to_all.25.reduce_sub_computation | reduce | bytes 1638402 | tf_op jit(solution)/shard_map/all_to_all | solution.py:28
  91.3 5.2 %all_to_all.33 = bf16[16,1,25600]{2,1,0:T(2,128)(2,1)S(1)} reshape(bf16[16,4,16,400]{3,2,1,0:T(8,128)(2,1)} %copy.37) | data formatting | bytes 1638400 | tf_op jit(solution)/shard_map/all_to_all | solution.py:28
  96.6 6.5 %reduce.5 = bf16[16,25600]{1,0:T(8,128)(2,1)} reduce(bf16[16,1,25600]{2,1,0:T(2,128)(2,1)S(1)} %all_to_all.33, bf16[]{:T(256)} %broadcast.92), dimensions={1}, to_apply=%all_to_all.33.reduce_sub_computation | reduce | bytes 1638402 | tf_op jit(solution)/shard_map/all_to_all | solution.py:28
  105.7 15.8 %all-to-all-start.1 = ((bf16[16,2,12800]{2,1,0:T(2,128)(2,1)}), bf16[16,2,12800]{2,1,0:T(2,128)(2,1)}, u32[]{:S(2)}, u32[]{:S(2)}) async-start(bf16[16,2,12800]{2,1,0:T(2,128)(2,1)} %reshape.222), calls=%async_computation.1 | async-start | bytes 1638400 | tf_op jit(solution)/shard_map/all_to_all | solution.py:28
  122.9 4.8 collective-permute-start.2
  127.7 8.4 %collective-permute-done.2 = bf16[1600,128]{1,0:T(8,128)(2,1)S(1)} collective-permute-done((bf16[1600,128]{1,0:T(8,128)(2,1)S(1)}, bf16[1600,128]{1,0:T(8,128)(2,1)S(1)}, u32[]{:S(2)}, u32[]{:S(2)}) %collective-permute-start.2) | collective-permute-done | bytes 409632 | tf_op jit(solution)/shard_map/ppermute | solution.py:16
  138.5 28.1 %collective-permute-done.3 = bf16[1600,128]{1,0:T(8,128)(2,1)S(1)} collective-permute-done((bf16[1600,128]{1,0:T(8,128)(2,1)S(1)}, bf16[1600,128]{1,0:T(8,128)(2,1)S(1)}, u32[]{:S(2)}, u32[]{:S(2)}) %collective-permute-start.3) | collective-permute-done | bytes 409632 | tf_op jit(solution)/shard_map/ppermute | solution.py:16
  166.7 5.2 %collective-permute-start.4 = (bf16[1600,128]{1,0:T(8,128)(2,1)S(1)}, bf16[1600,128]{1,0:T(8,128)(2,1)}, u32[]{:S(2)}, u32[]{:S(2)}) collective-permute-start(bf16[1600,128]{1,0:T(8,128)(2,1)S(1)} %add_convert_fusion.5), channel_id=1, source_target_pairs={{0,16},{1,17},{2,18},{3,19},{4,20},{5,21},{6,22},{7,23},{8,24},{9,... | collective-permute-start | bytes 1228808 | tf_op jit(solution)/shard_map/ppermute | solution.py:16
  177.6 12.4 %collective-permute-done.4 = bf16[1600,128]{1,0:T(8,128)(2,1)} collective-permute-done((bf16[1600,128]{1,0:T(8,128)(2,1)S(1)}, bf16[1600,128]{1,0:T(8,128)(2,1)}, u32[]{:S(2)}, u32[]{:S(2)}) %collective-permute-start.4) | collective-permute-done | bytes 409632 | tf_op jit(solution)/shard_map/ppermute | solution.py:16
  197.4 5.8 %reduce.1 = bf16[16,25600]{1,0:T(8,128)(2,1)} reduce(bf16[16,1,25600]{2,1,0:T(2,128)(2,1)S(1)} %reshape.223, bf16[]{:T(256)} %constant.24), dimensions={1}, to_apply=%all_to_all.27.reduce_sub_computation | reduce | bytes 1638402 | tf_op jit(solution)/shard_map/all_to_all | solution.py:28
  212.5 6.1 %all_to_all.34 = bf16[16,1,25600]{2,1,0:T(2,128)(2,1)} reshape(bf16[1024,400]{1,0:T(8,128)(2,1)} %copy.43) | data formatting | bytes 1638400 | tf_op jit(solution)/shard_map/all_to_all | solution.py:28
  218.6 6.6 %reduce.6 = bf16[16,25600]{1,0:T(8,128)(2,1)S(1)} reduce(bf16[16,1,25600]{2,1,0:T(2,128)(2,1)} %all_to_all.34, bf16[]{:T(256)} %broadcast.92), dimensions={1}, to_apply=%all_to_all.34.reduce_sub_computation | reduce | bytes 1638402 | tf_op jit(solution)/shard_map/all_to_all | solution.py:28
  226.7 12.6 %all-to-all-start.2 = ((bf16[16,2,12800]{2,1,0:T(2,128)(2,1)}), bf16[16,2,12800]{2,1,0:T(2,128)(2,1)S(1)}, u32[]{:S(2)}, u32[]{:S(2)}) async-start(bf16[16,2,12800]{2,1,0:T(2,128)(2,1)} %reshape.224), calls=%async_computation.2 | async-start | bytes 1638400 | tf_op jit(solution)/shard_map/all_to_all | solution.py:28
  255.7 9.3 %collective-permute-done.11 = bf16[1600,128]{1,0:T(8,128)(2,1)S(1)} collective-permute-done((bf16[1600,128]{1,0:T(8,128)(2,1)S(1)}, bf16[1600,128]{1,0:T(8,128)(2,1)S(1)}, u32[]{:S(2)}, u32[]{:S(2)}) %collective-permute-start.11) | collective-permute-done | bytes 409632 | tf_op jit(solution)/shard_map/ppermute | solution.py:16
  265.9 4.8 collective-permute-start.12
  270.7 12.4 %all-to-all-done.2 = bf16[16,2,12800]{2,1,0:T(2,128)(2,1)S(1)} async-done(((bf16[16,2,12800]{2,1,0:T(2,128)(2,1)}), bf16[16,2,12800]{2,1,0:T(2,128)(2,1)S(1)}, u32[]{:S(2)}, u32[]{:S(2)}) %all-to-all-start.2) | async-done | bytes 819232 | tf_op jit(solution)/shard_map/all_to_all | solution.py:28
  285.3 6.0 %reduce.2 = bf16[16,25600]{1,0:T(8,128)(2,1)S(1)} reduce(bf16[16,1,25600]{2,1,0:T(2,128)(2,1)} %reshape.225, bf16[]{:T(256)} %constant.24), dimensions={1}, to_apply=%all_to_all.29.reduce_sub_computation | reduce | bytes 1638402 | tf_op jit(solution)/shard_map/all_to_all | solution.py:28
  297.6 6.3 %all_to_all.35 = bf16[16,1,25600]{2,1,0:T(2,128)(2,1)} reshape(bf16[16,4,16,400]{3,2,1,0:T(8,128)(2,1)} %copy.46) | data formatting | bytes 1638400 | tf_op jit(solution)/shard_map/all_to_all | solution.py:28
  303.9 6.6 %reduce.7 = bf16[16,25600]{1,0:T(8,128)(2,1)S(1)} reduce(bf16[16,1,25600]{2,1,0:T(2,128)(2,1)} %all_to_all.35, bf16[]{:T(256)} %broadcast.92), dimensions={1}, to_apply=%all_to_all.35.reduce_sub_computation | reduce | bytes 1638402 | tf_op jit(solution)/shard_map/all_to_all | solution.py:28
  319.5 40.2 %collective-permute-done.13 = bf16[1600,128]{1,0:T(8,128)(2,1)S(1)} collective-permute-done((bf16[1600,128]{1,0:T(8,128)(2,1)S(1)}, bf16[1600,128]{1,0:T(8,128)(2,1)S(1)}, u32[]{:S(2)}, u32[]{:S(2)}) %collective-permute-start.13) | collective-permute-done | bytes 409632 | tf_op jit(solution)/shard_map/ppermute | solution.py:16
  361.8 20.2 %collective-permute-done.14 = bf16[1600,128]{1,0:T(8,128)(2,1)S(1)} collective-permute-done((bf16[1600,128]{1,0:T(8,128)(2,1)S(1)}, bf16[1600,128]{1,0:T(8,128)(2,1)S(1)}, u32[]{:S(2)}, u32[]{:S(2)}) %collective-permute-start.14) | collective-permute-done | bytes 409632 | tf_op jit(solution)/shard_map/ppermute | solution.py:16
  394.2 4.6 reshape.227
  398.9 5.8 %reduce.3 = bf16[16,25600]{1,0:T(8,128)(2,1)} reduce(bf16[16,1,25600]{2,1,0:T(2,128)(2,1)S(1)} %reshape.227, bf16[]{:T(256)} %constant.24), dimensions={1}, to_apply=%all_to_all.31.reduce_sub_computation | reduce | bytes 1638402 | tf_op jit(solution)/shard_map/all_to_all | solution.py:28
  429.6 18.2 %collective-permute-done.17 = bf16[800,128]{1,0:T(8,128)(2,1)S(1)} collective-permute-done((bf16[800,128]{1,0:T(8,128)(2,1)S(1)}, bf16[800,128]{1,0:T(8,128)(2,1)S(1)}, u32[]{:S(2)}, u32[]{:S(2)}) %collective-permute-start.17) | collective-permute-done | bytes 204832 | tf_op jit(solution)/shard_map/ppermute | solution.py:16
  447.9 8.2 %collective-permute-start.18 = (bf16[800,128]{1,0:T(8,128)(2,1)S(1)}, bf16[800,128]{1,0:T(8,128)(2,1)S(1)}, u32[]{:S(2)}, u32[]{:S(2)}) collective-permute-start(bf16[800,128]{1,0:T(8,128)(2,1)S(1)} %add_convert_fusion.10), channel_id=1, source_target_pairs={{0,256},{32,288},{64,320},{96,352},{128,384},{160,416},{192,448},{... | collective-permute-start | bytes 614408 | tf_op jit(solution)/shard_map/ppermute | solution.py:16
  458.1 19.1 %collective-permute-done.18 = bf16[800,128]{1,0:T(8,128)(2,1)S(1)} collective-permute-done((bf16[800,128]{1,0:T(8,128)(2,1)S(1)}, bf16[800,128]{1,0:T(8,128)(2,1)S(1)}, u32[]{:S(2)}, u32[]{:S(2)}) %collective-permute-start.18) | collective-permute-done | bytes 204832 | tf_op jit(solution)/shard_map/ppermute | solution.py:16
  484.6 4.7 collective-permute-done.9
  (128 shorter events, 140.0 us)
Async XLA Ops:
  0.6 88.7 %copy-start = (bf16[4,400,400]{2,1,0:T(8,128)(2,1)S(1)}, bf16[4,400,400]{2,1,0:T(8,128)(2,1)}, u32[]{:S(2)}) copy-start(bf16[4,400,400]{2,1,0:T(8,128)(2,1)} %param.7) | copy-start | bytes 3840004
  19.6 21.0 %copy-start.9 = (s32[1,2]{1,0:T(1,128)S(1)}, s32[1,2]{1,0:T(1,128)}, u32[]{:S(2)}) copy-start(s32[1,2]{1,0:T(1,128)} %param.13) | copy-start | bytes 28
  19.7 22.9 %copy-start.6 = (bf16[256,400]{0,1:T(8,128)(2,1)S(1)}, bf16[256,400]{0,1:T(8,128)(2,1)}, u32[]{:S(2)}) copy-start(bf16[256,400]{0,1:T(8,128)(2,1)} %param.9) | copy-start | bytes 614404
  22.4 53.2 %all-to-all-start = ((bf16[16,2,12800]{2,1,0:T(2,128)(2,1)}), bf16[16,2,12800]{2,1,0:T(2,128)(2,1)}, u32[]{:S(2)}, u32[]{:S(2)}) async-start(bf16[16,2,12800]{2,1,0:T(2,128)(2,1)} %reshape.220), calls=%async_computation | async-start | bytes 1638400 | tf_op jit(solution)/shard_map/all_to_all | solution.py:28
  43.9 4.2 collective-permute-start
  49.0 72.6 %collective-permute-start.1 = (bf16[1600,128]{1,0:T(8,128)(2,1)}, bf16[1600,128]{1,0:T(8,128)(2,1)}, u32[]{:S(2)}, u32[]{:S(2)}) collective-permute-start(bf16[1600,128]{1,0:T(8,128)(2,1)} %add_convert_fusion.8), channel_id=1, source_target_pairs={{0,2},{1,3},{2,0},{3,1},{4,6},{5,7},{6,4},{7,5},{8,10},{9,11},{10,... | collective-permute-start | bytes 1228808 | tf_op jit(solution)/shard_map/ppermute | solution.py:16
  105.7 87.3 %all-to-all-start.1 = ((bf16[16,2,12800]{2,1,0:T(2,128)(2,1)}), bf16[16,2,12800]{2,1,0:T(2,128)(2,1)}, u32[]{:S(2)}, u32[]{:S(2)}) async-start(bf16[16,2,12800]{2,1,0:T(2,128)(2,1)} %reshape.222), calls=%async_computation.1 | async-start | bytes 1638400 | tf_op jit(solution)/shard_map/all_to_all | solution.py:28
  121.6 16.7 %copy-start.10 = (s32[1,1,64]{2,1,0:T(1,128)S(1)}, s32[1,1,64]{2,1,0:T(1,128)}, u32[]{:S(2)}) copy-start(s32[1,1,64]{2,1,0:T(1,128)} %param.12) | copy-start | bytes 772
  122.9 49.1 %copy-start.7 = (s32[1,1,1024]{2,1,0:T(1,128)S(1)}, s32[1,1,1024]{2,1,0:T(1,128)}, u32[]{:S(2)}) copy-start(s32[1,1,1024]{2,1,0:T(1,128)} %param.11) | copy-start | bytes 12292
  122.9 13.2 %collective-permute-start.2 = (bf16[1600,128]{1,0:T(8,128)(2,1)S(1)}, bf16[1600,128]{1,0:T(8,128)(2,1)S(1)}, u32[]{:S(2)}, u32[]{:S(2)}) collective-permute-start(bf16[1600,128]{1,0:T(8,128)(2,1)S(1)} %add_convert_fusion.7), channel_id=1, source_target_pairs={{0,4},{1,5},{2,6},{3,7},{4,0},{5,1},{6,2},{7,3},{8,12},{9,13},{10,... | collective-permute-start | bytes 1228808 | tf_op jit(solution)/shard_map/ppermute | solution.py:16
  136.2 30.4 %collective-permute-start.3 = (bf16[1600,128]{1,0:T(8,128)(2,1)S(1)}, bf16[1600,128]{1,0:T(8,128)(2,1)S(1)}, u32[]{:S(2)}, u32[]{:S(2)}) collective-permute-start(bf16[1600,128]{1,0:T(8,128)(2,1)S(1)} %add_convert_fusion.6), channel_id=1, source_target_pairs={{0,8},{1,9},{2,10},{3,11},{4,12},{5,13},{6,14},{7,15},{8,0},{9,1},... | collective-permute-start | bytes 1228808 | tf_op jit(solution)/shard_map/ppermute | solution.py:16
  166.7 23.2 %collective-permute-start.4 = (bf16[1600,128]{1,0:T(8,128)(2,1)S(1)}, bf16[1600,128]{1,0:T(8,128)(2,1)}, u32[]{:S(2)}, u32[]{:S(2)}) collective-permute-start(bf16[1600,128]{1,0:T(8,128)(2,1)S(1)} %add_convert_fusion.5), channel_id=1, source_target_pairs={{0,16},{1,17},{2,18},{3,19},{4,20},{5,21},{6,22},{7,23},{8,24},{9,... | collective-permute-start | bytes 1228808 | tf_op jit(solution)/shard_map/ppermute | solution.py:16
  207.2 1.9 copy-start.2
  209.1 1.4 copy-start.3
  226.7 56.5 %all-to-all-start.2 = ((bf16[16,2,12800]{2,1,0:T(2,128)(2,1)}), bf16[16,2,12800]{2,1,0:T(2,128)(2,1)S(1)}, u32[]{:S(2)}, u32[]{:S(2)}) async-start(bf16[16,2,12800]{2,1,0:T(2,128)(2,1)} %reshape.224), calls=%async_computation.2 | async-start | bytes 1638400 | tf_op jit(solution)/shard_map/all_to_all | solution.py:28
  247.1 4.2 collective-permute-start.10
  252.5 12.5 %collective-permute-start.11 = (bf16[1600,128]{1,0:T(8,128)(2,1)S(1)}, bf16[1600,128]{1,0:T(8,128)(2,1)S(1)}, u32[]{:S(2)}, u32[]{:S(2)}) collective-permute-start(bf16[1600,128]{1,0:T(8,128)(2,1)S(1)} %add_convert_fusion.3), channel_id=1, source_target_pairs={{0,2},{1,3},{2,0},{3,1},{4,6},{5,7},{6,4},{7,5},{8,10},{9,11},{10,... | collective-permute-start | bytes 1228808 | tf_op jit(solution)/shard_map/ppermute | solution.py:16
  265.9 50.5 %collective-permute-start.12 = (bf16[1600,128]{1,0:T(8,128)(2,1)}, bf16[1600,128]{1,0:T(8,128)(2,1)}, u32[]{:S(2)}, u32[]{:S(2)}) collective-permute-start(bf16[1600,128]{1,0:T(8,128)(2,1)} %add_convert_fusion.2), channel_id=1, source_target_pairs={{0,4},{1,5},{2,6},{3,7},{4,0},{5,1},{6,2},{7,3},{8,12},{9,13},{10,... | collective-permute-start | bytes 1228808 | tf_op jit(solution)/shard_map/ppermute | solution.py:16
  312.0 82.2 %all-to-all-start.3 = ((bf16[16,2,12800]{2,1,0:T(2,128)(2,1)}), bf16[16,2,12800]{2,1,0:T(2,128)(2,1)}, u32[]{:S(2)}, u32[]{:S(2)}) async-start(bf16[16,2,12800]{2,1,0:T(2,128)(2,1)} %reshape.226), calls=%async_computation.3 | async-start | bytes 1638400 | tf_op jit(solution)/shard_map/all_to_all | solution.py:28
  317.6 42.2 %collective-permute-start.13 = (bf16[1600,128]{1,0:T(8,128)(2,1)S(1)}, bf16[1600,128]{1,0:T(8,128)(2,1)S(1)}, u32[]{:S(2)}, u32[]{:S(2)}) collective-permute-start(bf16[1600,128]{1,0:T(8,128)(2,1)S(1)} %add_convert_fusion.1), channel_id=1, source_target_pairs={{0,8},{1,9},{2,10},{3,11},{4,12},{5,13},{6,14},{7,15},{8,0},{9,1},... | collective-permute-start | bytes 1228808 | tf_op jit(solution)/shard_map/ppermute | solution.py:16
  359.9 22.1 %collective-permute-start.14 = (bf16[1600,128]{1,0:T(8,128)(2,1)S(1)}, bf16[1600,128]{1,0:T(8,128)(2,1)S(1)}, u32[]{:S(2)}, u32[]{:S(2)}) collective-permute-start(bf16[1600,128]{1,0:T(8,128)(2,1)S(1)} %add_convert_fusion), channel_id=1, source_target_pairs={{0,16},{1,17},{2,18},{3,19},{4,20},{5,21},{6,22},{7,23},{8,24},{9,... | collective-permute-start | bytes 1228808 | tf_op jit(solution)/shard_map/ppermute | solution.py:16
  391.1 21.8 %collective-permute-start.15 = (bf16[800,128]{1,0:T(8,128)(2,1)S(1)}, bf16[800,128]{1,0:T(8,128)(2,1)}, u32[]{:S(2)}, u32[]{:S(2)}) collective-permute-start(bf16[800,128]{1,0:T(8,128)(2,1)S(1)} %convert_element_type.298), channel_id=1, source_target_pairs={{0,32},{32,0},{64,96},{96,64},{128,160},{160,128},{192,224},{224,1... | collective-permute-start | bytes 614408 | tf_op jit(solution)/shard_map/ppermute | solution.py:16
  398.8 9.3 %copy-start.8 = (s32[1,1,1024]{2,1,0:T(1,128)S(1)}, s32[1,1,1024]{2,1,0:T(1,128)}, u32[]{:S(2)}) copy-start(s32[1,1,1024]{2,1,0:T(1,128)} %param.10) | copy-start | bytes 12292
  409.4 8.9 %collective-permute-start.5 = (bf16[800,128]{1,0:T(8,128)(2,1)S(1)}, bf16[800,128]{1,0:T(8,128)(2,1)S(1)}, u32[]{:S(2)}, u32[]{:S(2)}) collective-permute-start(bf16[800,128]{1,0:T(8,128)(2,1)S(1)} %convert_element_type.264), channel_id=1, source_target_pairs={{0,1},{1,0},{2,3},{3,2},{4,5},{5,4},{6,7},{7,6},{8,9},{9,8},{10,11... | collective-permute-start | bytes 614408 | tf_op jit(solution)/shard_map/ppermute | solution.py:16
  413.9 10.0 %collective-permute-start.16 = (bf16[800,128]{1,0:T(8,128)(2,1)S(1)}, bf16[800,128]{1,0:T(8,128)(2,1)S(1)}, u32[]{:S(2)}, u32[]{:S(2)}) collective-permute-start(bf16[800,128]{1,0:T(8,128)(2,1)S(1)} %add_convert_fusion.12), channel_id=1, source_target_pairs={{0,64},{32,96},{64,0},{96,32},{128,192},{160,224},{192,128},{224,1... | collective-permute-start | bytes 614408 | tf_op jit(solution)/shard_map/ppermute | solution.py:16
  418.3 8.8 %collective-permute-start.6 = (bf16[800,128]{1,0:T(8,128)(2,1)S(1)}, bf16[800,128]{1,0:T(8,128)(2,1)S(1)}, u32[]{:S(2)}, u32[]{:S(2)}) collective-permute-start(bf16[800,128]{1,0:T(8,128)(2,1)S(1)} %add_convert_fusion.17), channel_id=1, source_target_pairs={{0,2},{1,3},{2,0},{3,1},{4,6},{5,7},{6,4},{7,5},{8,10},{9,11},{10,... | collective-permute-start | bytes 614408 | tf_op jit(solution)/shard_map/ppermute | solution.py:16
  424.0 23.8 %collective-permute-start.17 = (bf16[800,128]{1,0:T(8,128)(2,1)S(1)}, bf16[800,128]{1,0:T(8,128)(2,1)S(1)}, u32[]{:S(2)}, u32[]{:S(2)}) collective-permute-start(bf16[800,128]{1,0:T(8,128)(2,1)S(1)} %add_convert_fusion.11), channel_id=1, source_target_pairs={{0,128},{32,160},{64,192},{96,224},{128,0},{160,32},{192,64},{224,... | collective-permute-start | bytes 614408 | tf_op jit(solution)/shard_map/ppermute | solution.py:16
  427.2 54.4 %copy-start.5 = (bf16[16,4,16,400]{3,2,1,0:T(8,128)(2,1)S(1)}, bf16[16,4,16,400]{3,2,1,0:T(8,128)(2,1)}, u32[]{:S(2)}) copy-start(bf16[16,4,16,400]{3,2,1,0:T(8,128)(2,1)} %copy-done.4) | copy-start | bytes 2457604
  427.2 28.9 %collective-permute-start.7 = (bf16[800,128]{1,0:T(8,128)(2,1)S(1)}, bf16[800,128]{1,0:T(8,128)(2,1)S(1)}, u32[]{:S(2)}, u32[]{:S(2)}) collective-permute-start(bf16[800,128]{1,0:T(8,128)(2,1)S(1)} %add_convert_fusion.16), channel_id=1, source_target_pairs={{0,4},{1,5},{2,6},{3,7},{4,0},{5,1},{6,2},{7,3},{8,12},{9,13},{10,... | collective-permute-start | bytes 614408 | tf_op jit(solution)/shard_map/ppermute | solution.py:16
  447.9 29.3 %collective-permute-start.18 = (bf16[800,128]{1,0:T(8,128)(2,1)S(1)}, bf16[800,128]{1,0:T(8,128)(2,1)S(1)}, u32[]{:S(2)}, u32[]{:S(2)}) collective-permute-start(bf16[800,128]{1,0:T(8,128)(2,1)S(1)} %add_convert_fusion.10), channel_id=1, source_target_pairs={{0,256},{32,288},{64,320},{96,352},{128,384},{160,416},{192,448},{... | collective-permute-start | bytes 614408 | tf_op jit(solution)/shard_map/ppermute | solution.py:16
  456.2 22.4 %collective-permute-start.8 = (bf16[800,128]{1,0:T(8,128)(2,1)S(1)}, bf16[800,128]{1,0:T(8,128)(2,1)}, u32[]{:S(2)}, u32[]{:S(2)}) collective-permute-start(bf16[800,128]{1,0:T(8,128)(2,1)S(1)} %add_convert_fusion.15), channel_id=1, source_target_pairs={{0,8},{1,9},{2,10},{3,11},{4,12},{5,13},{6,14},{7,15},{8,0},{9,1},... | collective-permute-start | bytes 614408 | tf_op jit(solution)/shard_map/ppermute | solution.py:16
  479.6 9.7 %collective-permute-start.9 = (bf16[800,128]{1,0:T(8,128)(2,1)S(1)}, bf16[800,128]{1,0:T(8,128)(2,1)S(1)}, u32[]{:S(2)}, u32[]{:S(2)}) collective-permute-start(bf16[800,128]{1,0:T(8,128)(2,1)S(1)} %add_convert_fusion.14), channel_id=1, source_target_pairs={{0,16},{1,17},{2,18},{3,19},{4,20},{5,21},{6,22},{7,23},{8,24},{9,... | collective-permute-start | bytes 614408 | tf_op jit(solution)/shard_map/ppermute | solution.py:16
  (2 other events, 2.3 us)
